TPU v7x, 32 devices: a whole 2x2x4 slice. The times are simulated.
32 devices in a mesh: depth: 2 (over y), row: 4 (over x, core), col: 4 (over z).
Axes of the slice: x: 2, y: 2, z: 4, core: 2. Of those that a mesh axis runs over, the one named last changes fastest.
Arguments:
- tokens: bfloat16 [512, 16384], P('col', ('depth', 'row')), may hold values from -6 to 6
- weight: bfloat16 [16384, 26624], P(('depth', 'row'), 'col'), may hold values from -0.0625 to 0.0625
Outputs:
- hidden: bfloat16 [512, 4, 6656], P('row', 'col', 'depth')
All inputs are finite; a program needn't handle non-finite values.
Results may differ from a plain program's by a relative error of at most 0.001.
Values may be sent and summed in bfloat16 or wider, within the bound.
No kernel may reach another device: no remote copies, remote signals or barrier semaphores. Data moves between devices by JAX's collectives and lax.ppermute only.
A program may use at most 128 MiB of HBM per device.

v0:
```python
import jax
import jax.numpy as jnp
from jax import lax
from jax.sharding import PartitionSpec as P


def from_behind(value, axis, steps):
    count = lax.axis_size(axis)
    pairs = [(source, (source + steps) % count) for source in range(count)]
    return lax.ppermute(value, axis, pairs)


def local(tokens, weight):
    row_count = lax.axis_size("row")
    row_index = lax.axis_index("row")
    gathered = lax.all_gather(tokens, "col", axis=0, tiled=True)
    block_rows = gathered.shape[0] // row_count
    width = weight.shape[1]
    partial_value = jnp.zeros((block_rows, width), jnp.float32)
    for step in range(row_count):
        target = (row_index + 1 + step) % row_count
        rows_now = lax.dynamic_slice_in_dim(gathered, target * block_rows, block_rows, 0)
        partial_value = partial_value + jnp.dot(
            rows_now, weight, preferred_element_type=jnp.float32
        )
        if step + 1 < row_count:
            partial_value = from_behind(partial_value, "row", -1)
    shares = lax.psum_scatter(partial_value, "depth", scatter_dimension=1, tiled=True)
    return shares.astype(jnp.bfloat16).reshape(block_rows, 1, shares.shape[1])


def solution(mesh):
    in_specs = (P("col", ("depth", "row")), P(("depth", "row"), "col"))
    out_specs = P("row", "col", "depth")
    return jax.shard_map(local, mesh=mesh, in_specs=in_specs, out_specs=out_specs, check_vma=False)
```

profile of v0, /device:TPU:0, one launch (start us, length us, event | category | flops | bytes accessed | tf_op | source)
XLA Modules:
  0.0 261.7 jit_solution(4772752704282715040)
XLA Ops:
  6.5 0.0 all-gather.2.cloned.1.call-start
  6.5 0.7 all-gather.2.cloned.1.call-update
  7.3 0.0 reduce-scatter.2.cloned.1.call-start
  7.3 50.0 %all-gather.2.cloned.1.call-done = bf16[512,2048]{1,0:T(8,128)(2,1)} async-done(((bf16[128,2048]{1,0:T(8,128)(2,1)}), bf16[512,2048]{1,0:T(8,128)(2,1)}) %all-gather.2.cloned.1.call-update) | async-done | bytes 2097168 | tf_op jit(solution)/shard_map/all_gather | solution.py:16
  57.3 10.9 %fusion.5 = f32[128,6656]{1,0:T(8,128)S(1)} fusion(bf16[2048,6656]{1,0:T(8,128)(2,1)} %param.3, bf16[512,2048]{1,0:T(8,128)(2,1)} %all-gather.2.cloned.1.call-done, s32[]{:T(128)S(6)} %select_n.32), kind=kOutput, calls=%fused_computation.7 | convolution fusion | flops 3489660928 | bytes 31195140 | tf_op jit(solution)/shard_map/dot_general | solution.py:23
  68.2 0.8 collective-permute-start
  69.0 37.6 %collective-permute-done = f32[128,6656]{1,0:T(8,128)} collective-permute-done((f32[128,6656]{1,0:T(8,128)S(1)}, f32[128,6656]{1,0:T(8,128)}, u32[]{:S(2)}, u32[]{:S(2)}) %collective-permute-start) | collective-permute-done | bytes 3407904 | tf_op jit(solution)/shard_map/ppermute | solution.py:10
  106.6 13.6 %convolution_add_fusion = f32[128,6656]{1,0:T(8,128)S(1)} fusion(f32[128,6656]{1,0:T(8,128)} %collective-permute-done, bf16[2048,6656]{1,0:T(8,128)(2,1)} %param.3, bf16[512,2048]{1,0:T(8,128)(2,1)} %all-gather.2.cloned.1.call-done, s32[]{:T(128)S(6)} %select_n.34), kind=kOutput, calls=%fused_computation | convolution fusion | flops 3490512896 | bytes 34603012 | tf_op jit(solution)/shard_map/dot_general | solution.py:23
  120.2 2.1 collective-permute-start.1
  122.2 10.9 %fusion.2 = f32[128,6656]{1,0:T(8,128)S(1)} fusion(bf16[2048,6656]{1,0:T(8,128)(2,1)} %param.3, bf16[512,2048]{1,0:T(8,128)(2,1)} %all-gather.2.cloned.1.call-done, s32[]{:T(128)S(6)} %select_n.36), kind=kOutput, calls=%fused_computation.4 | convolution fusion | flops 3489660928 | bytes 31195140 | tf_op jit(solution)/shard_map/dot_general | solution.py:23
  133.1 26.7 %collective-permute-done.1 = f32[128,6656]{1,0:T(8,128)} collective-permute-done((f32[128,6656]{1,0:T(8,128)S(1)}, f32[128,6656]{1,0:T(8,128)}, u32[]{:S(2)}, u32[]{:S(2)}) %collective-permute-start.1) | collective-permute-done | bytes 3407904 | tf_op jit(solution)/shard_map/ppermute | solution.py:10
  159.8 2.5 add.67
  162.3 2.1 collective-permute-start.2
  164.4 10.9 %fusion = f32[128,6656]{1,0:T(8,128)S(1)} fusion(bf16[2048,6656]{1,0:T(8,128)(2,1)} %param.3, bf16[512,2048]{1,0:T(8,128)(2,1)} %all-gather.2.cloned.1.call-done, s32[]{:T(128)S(6)} %select_n.38), kind=kOutput, calls=%fused_computation.2 | convolution fusion | flops 3489660928 | bytes 31195140 | tf_op jit(solution)/shard_map/dot_general | solution.py:23
  175.3 26.7 %collective-permute-done.2 = f32[128,6656]{1,0:T(8,128)} collective-permute-done((f32[128,6656]{1,0:T(8,128)S(1)}, f32[128,6656]{1,0:T(8,128)}, u32[]{:S(2)}, u32[]{:S(2)}) %collective-permute-start.2) | collective-permute-done | bytes 3407904 | tf_op jit(solution)/shard_map/ppermute | solution.py:10
  202.0 4.3 %add.71 = f32[128,6656]{1,0:T(8,128)} add(f32[128,6656]{1,0:T(8,128)} %collective-permute-done.2, f32[128,6656]{1,0:T(8,128)S(1)} %fusion) | non-fusion elementwise | flops 851968 | bytes 10223616 | tf_op jit(solution)/shard_map/add | solution.py:23
  206.3 0.0 reduce-scatter.2.cloned.1.call-update
  206.3 46.1 %reduce-scatter.2.cloned.1.call-done = f32[128,3328]{1,0:T(8,128)} async-done(((f32[128,6656]{1,0:T(8,128)}), f32[128,3328]{1,0:T(8,128)}) %reduce-scatter.2.cloned.1.call-update) | async-done | bytes 1703952 | tf_op jit(solution)/shard_map/reduce_scatter | solution.py:28
  252.4 2.4 convert_bitcast_fusion
Async XLA Ops:
  6.5 50.8 %all-gather.2.cloned.1.call-start = ((), (), s32[]{:S(2)}) async-start(), calls=%async_computation.1 | async-start | bytes 2621440 | tf_op jit(solution)/shard_map/all_gather | solution.py:16
  7.3 245.1 %reduce-scatter.2.cloned.1.call-start = ((), (), s32[]{:S(2)}) async-start(), calls=%async_computation.2 | async-start | bytes 5111808 | tf_op jit(solution)/shard_map/reduce_scatter | solution.py:28
  68.2 38.4 %collective-permute-start = (f32[128,6656]{1,0:T(8,128)S(1)}, f32[128,6656]{1,0:T(8,128)}, u32[]{:S(2)}, u32[]{:S(2)}) collective-permute-start(f32[128,6656]{1,0:T(8,128)S(1)} %fusion.5), channel_id=1, source_target_pairs={{0,12},{4,0},{8,4},{12,8},{1,13},{5,1},{9,5},{13,9},{2,14},{6,2},{... | collective-permute-start | bytes 10223624 | tf_op jit(solution)/shard_map/ppermute | solution.py:10
  120.2 39.7 %collective-permute-start.1 = (f32[128,6656]{1,0:T(8,128)S(1)}, f32[128,6656]{1,0:T(8,128)}, u32[]{:S(2)}, u32[]{:S(2)}) collective-permute-start(f32[128,6656]{1,0:T(8,128)S(1)} %convolution_add_fusion), channel_id=1, source_target_pairs={{0,12},{4,0},{8,4},{12,8},{1,13},{5,1},{9,5},{13,9},{2,14},{6,2},{... | collective-permute-start | bytes 10223624 | tf_op jit(solution)/shard_map/ppermute | solution.py:10
  162.3 39.7 %collective-permute-start.2 = (f32[128,6656]{1,0:T(8,128)S(1)}, f32[128,6656]{1,0:T(8,128)}, u32[]{:S(2)}, u32[]{:S(2)}) collective-permute-start(f32[128,6656]{1,0:T(8,128)S(1)} %add.67), channel_id=1, source_target_pairs={{0,12},{4,0},{8,4},{12,8},{1,13},{5,1},{9,5},{13,9},{2,14},{6,2},{... | collective-permute-start | bytes 10223624 | tf_op jit(solution)/shard_map/ppermute | solution.py:10
Sparse Core Ops, SparseCore 0:
  8.9 48.3 all-gather.1
  206.4 45.9 reduce-scatter.1
where the time goes:
time: 262 us
  waiting for transfers between devices  188 us (72%)
  matrix products  46.2 us (18%)
  between operations  13.5 us (5%)
  other arithmetic  9.19 us (4%)
  starting transfers between devices  4.95 us (2%)
    ppermute x3, waiting for transfers between devices, from_behind(): return lax.ppermute(value, axis, pairs)  91 us
    all_gather x1, waiting for transfers between devices, local(): gathered = lax.all_gather(tokens, 'col', axis=0, tiled=True)  50 us
    dot_general x4, matrix products, local(): jnp.dot(rows_now, weight, preferred_element_type=jnp.float32)  46.2 us
    reduce_scatter x1, waiting for transfers between devices, local(): lax.psum_scatter(partial_value, 'depth', scatter_dimension=1, tiled=True)  46.1 us
    add x2, other arithmetic, local(): partial_value + jnp.dot(rows_now, weight, preferred_element_type=jnp.floa...  6.74 us
  transfers between devices with their start and end apart: 5, of which 5 were waited for; matrix products, arithmetic and copies ran while one was open for 8% of the time, Pallas kernels for 0%

commit v1 on v0

v1 whole, which is shorter than its diff:
```python
import jax
import jax.numpy as jnp
from jax import lax
from jax.sharding import PartitionSpec as P


def ring_reduce_scatter(x, dim, size, index, shift):
    if size == 1:
        return lax.index_in_dim(x, 0, dim, keepdims=False)
    buf = lax.dynamic_index_in_dim(x, (index - 1) % size, dim, keepdims=False)
    for step in range(size - 1):
        received = shift(buf)
        chunk = (index - step - 2) % size
        buf = received + lax.dynamic_index_in_dim(x, chunk, dim, keepdims=False)
    return buf


def local(tokens, weight):
    n_row = lax.axis_size("row")
    n_depth = lax.axis_size("depth")
    row = lax.axis_index("row")
    depth = lax.axis_index("depth")
    core = row % 2
    hi = row // 2
    n_hi = n_row // 2

    gathered = lax.all_gather(tokens, "col", axis=0, tiled=True)
    product = jnp.dot(gathered, weight, preferred_element_type=jnp.float32)
    total, width = product.shape
    block = total // n_row
    part = width // n_depth
    product = product.reshape(n_hi, 2, block, n_depth, part)

    keep = lax.dynamic_index_in_dim(product, core, 1, keepdims=False)
    send = lax.dynamic_index_in_dim(product, 1 - core, 1, keepdims=False)
    partner = [(q, q ^ 1) for q in range(n_row)]
    summed = keep + lax.ppermute(send, "row", partner)

    def shift_hi(value):
        pairs = [(h * 2 + c, ((h + 1) % n_hi) * 2 + c) for h in range(n_hi) for c in range(2)]
        return lax.ppermute(value, "row", pairs)

    def shift_depth(value):
        pairs = [(q, (q + 1) % n_depth) for q in range(n_depth)]
        return lax.ppermute(value, "depth", pairs)

    half = block // 2
    first = summed[:, :half]
    second = summed[:, half:]
    first = ring_reduce_scatter(first, 0, n_hi, hi, shift_hi)
    first = ring_reduce_scatter(first, 1, n_depth, depth, shift_depth)
    second = ring_reduce_scatter(second, 2, n_depth, depth, shift_depth)
    second = ring_reduce_scatter(second, 0, n_hi, hi, shift_hi)
    shares = jnp.concatenate([first, second], axis=0)
    return shares.astype(jnp.bfloat16).reshape(block, 1, part)


def solution(mesh):
    in_specs = (P("col", ("depth", "row")), P(("depth", "row"), "col"))
    out_specs = P("row", "col", "depth")
    return jax.shard_map(local, mesh=mesh, in_specs=in_specs, out_specs=out_specs, check_vma=False)
```

time: 262 us -> 202 us (0.77)
  waiting for transfers between devices: 188 us -> 116 us
  local copies, waits for them, and re-layouts: 0 us -> 33.4 us
  matrix products: 46.2 us -> 22.8 us
    reduce_scatter x1 -> x0, waiting for transfers between devices: 46.1 us -> none  [local(): lax.psum_scatter(partial_value, 'depth', scatter_dimension=1, tiled=True)]
    ppermute x3 -> x5, waiting for transfers between devices: 91 us -> 64.8 us  [the longest x2 35.3 us: shift_hi(): return lax.ppermute(value, 'row', pairs)]
    dot_general x4 -> x1, matrix products: 46.2 us -> 22.8 us  [local(): product = jnp.dot(gathered, weight, preferred_element_type=jnp.float32)]
    reshape x0 -> x1, local copies, waits for them, and re-layouts: none -> 17 us  [local(): product = product.reshape(n_hi, 2, block, n_depth, part)]
    squeeze x0 -> x3, local copies, waits for them, and re-layouts: none -> 8.21 us  [the longest x1 8.08 us: local(): send = lax.dynamic_index_in_dim(product, 1 - core, 1, keepdims=False)]
    dynamic_slice x0 -> x3, local copies, waits for them, and re-layouts: none -> 5.72 us  [the longest x2 4.4 us: ring_reduce_scatter(): buf = received + lax.dynamic_index_in_dim(x, chunk, dim, keepdims=False)]
    add x2 -> x3, other arithmetic: 6.74 us -> 9.65 us  [the longest x1 7.81 us: local(): summed = keep + lax.ppermute(send, 'row', partner)]
  transfers between devices with their start and end apart: 5 -> 6, of which waited for: 5 -> 6; matrix products, arithmetic and copies ran while one was open for 8% -> 3% of each run, Pallas kernels for 0% -> 0%
where the time goes in v1:
time: 202 us; the launch traced here: 201 us
  waiting for transfers between devices  116 us (57%)
  local copies, waits for them, and re-layouts  33.4 us (17%)
  matrix products  22.8 us (11%)
  between operations  13.5 us (7%)
  other arithmetic  10.8 us (5%)
  starting transfers between devices  5.02 us (2%)
    all_gather x1, waiting for transfers between devices, local(): gathered = lax.all_gather(tokens, 'col', axis=0, tiled=True)  50 us
    ppermute x2, waiting for transfers between devices, shift_hi(): return lax.ppermute(value, 'row', pairs)  35.3 us
    dot_general x1, matrix products, local(): product = jnp.dot(gathered, weight, preferred_element_type=jnp.float32)  22.8 us
    ppermute x2, waiting for transfers between devices, shift_depth(): return lax.ppermute(value, 'depth', pairs)  18.3 us
    reshape x1, local copies, waits for them, and re-layouts, local(): product = product.reshape(n_hi, 2, block, n_depth, part)  17 us
    ppermute x1, waiting for transfers between devices, local(): summed = keep + lax.ppermute(send, 'row', partner)  11.2 us
    squeeze x1, local copies, waits for them, and re-layouts, local(): send = lax.dynamic_index_in_dim(product, 1 - core, 1, keepdims=False)  8.08 us
    add x1, other arithmetic, local(): summed = keep + lax.ppermute(send, 'row', partner)  7.81 us
  transfers between devices with their start and end apart: 6, of which 6 were waited for; matrix products, arithmetic and copies ran while one was open for 3% of the time, Pallas kernels for 0%

profile of v1, /device:TPU:0, one launch (start us, length us, event | category | flops | bytes accessed | tf_op | source)
XLA Modules:
  0.0 201.1 jit_solution(8557466065578642722)
XLA Ops:
  6.5 0.7 all-gather.2.cloned.1.call-update
  7.3 50.0 %all-gather.2.cloned.1.call-done = bf16[512,2048]{1,0:T(8,128)(2,1)} async-done(((bf16[128,2048]{1,0:T(8,128)(2,1)}), bf16[512,2048]{1,0:T(8,128)(2,1)}) %all-gather.2.cloned.1.call-update) | async-done | bytes 2097168 | tf_op jit(solution)/shard_map/all_gather | solution.py:27
  57.3 22.8 %fusion.5 = f32[512,6656]{1,0:T(8,128)} fusion(bf16[512,2048]{1,0:T(8,128)(2,1)} %all-gather.2.cloned.1.call-done, bf16[2048,6656]{1,0:T(8,128)(2,1)} %param.3), kind=kOutput, calls=%fused_computation.20 | convolution fusion | flops 13958643712 | bytes 42991616 | tf_op jit(solution)/shard_map/dot_general | solution.py:28
  80.1 17.0 %reshape.35 = f32[2,2,128,2,3328]{4,3,2,1,0:T(2,128)} reshape(f32[512,6656]{1,0:T(8,128)} %fusion.5) | data formatting | bytes 27262976 | tf_op jit(solution)/shard_map/reshape | solution.py:32
  97.2 8.1 %dynamic-slice_bitcast_fusion = f32[2,128,2,3328]{3,2,1,0:T(2,128)} fusion(f32[2,2,128,2,3328]{4,3,2,1,0:T(2,128)} %reshape.35, s32[]{:T(128)S(6)} %select_n.64), kind=kLoop, calls=%fused_computation.1 | loop fusion | bytes 13631492 | tf_op jit(solution)/shard_map/jit(dynamic_index_in_dim)/squeeze | solution.py:35
  105.2 11.2 %collective-permute-done = f32[2,128,2,3328]{3,2,1,0:T(2,128)} collective-permute-done((f32[2,128,2,3328]{3,2,1,0:T(2,128)}, f32[2,128,2,3328]{3,2,1,0:T(2,128)}, u32[]{:S(2)}, u32[]{:S(2)}) %collective-permute-start) | collective-permute-done | bytes 6815776 | tf_op jit(solution)/shard_map/ppermute | solution.py:37
  116.5 7.8 %bitcast_add_fusion = f32[2,128,2,3328]{3,2,1,0:T(2,128)S(1)} fusion(f32[2,128,2,3328]{3,2,1,0:T(2,128)} %collective-permute-done, f32[2,2,128,2,3328]{4,3,2,1,0:T(2,128)} %reshape.35, s32[]{:T(128)S(6)} %select_n.63), kind=kLoop, calls=%fused_computation | loop fusion | flops 1703936 | bytes 20447236 | tf_op jit(solution)/shard_map/add | solution.py:37
  124.3 2.3 %fusion.4 = (f32[2,64,2,3328]{3,2,1,0:T(2,128)S(1)}, f32[2,64,2,3328]{3,2,1,0:T(2,128)S(1)}) fusion(f32[2,128,2,3328]{3,2,1,0:T(2,128)S(1)} %bitcast_add_fusion), kind=kLoop, calls=%fused_computation.19 | loop fusion | bytes 13631488 | tf_op jit(solution)/shard_map/slice | solution.py:48
  126.7 1.5 constant_dynamic-slice_fusion.2
  128.1 1.3 copy.12
  129.5 1.5 collective-permute-start.1
  130.9 2.9 %constant_dynamic-slice_fusion = (f32[2,64,1,3328]{3,2,1,0:T(1,128)S(1)}, f32[2,64,1,3328]{3,2,1,0:T(1,128)S(1)}) fusion(f32[2,64,2,3328]{3,2,1,0:T(2,128)S(1)} %get-tuple-element.6, s32[]{:T(128)S(6)} %select_n.73, s32[]{:T(128)S(6)} %select_n.71), kind=kLoop, calls=%fused_computation.15 | loop fusion | bytes 6815752 | tf_op jit(solution)/shard_map/jit(dynamic_index_in_dim)/dynamic_slice | solution.py:14
  133.9 0.1 copy.11
  134.0 1.5 collective-permute-start.3
  135.5 33.5 %collective-permute-done.1 = f32[64,2,3328]{2,0,1:T(8,128)} collective-permute-done((f32[64,2,3328]{2,0,1:T(8,128)}, f32[64,2,3328]{2,0,1:T(8,128)}, u32[]{:S(2)}, u32[]{:S(2)}) %collective-permute-start.1) | collective-permute-done | bytes 1703968 | tf_op jit(solution)/shard_map/ppermute | solution.py:41
  169.0 1.6 bitcast_add_fusion.2
  170.7 1.5 collective-permute-start.2
  172.3 1.1 collective-permute-done.3
  173.4 0.2 bitcast_add_fusion.1
  173.6 0.5 collective-permute-start.4
  174.1 17.2 %collective-permute-done.2 = f32[64,3328]{1,0:T(8,128)S(1)} collective-permute-done((f32[64,3328]{1,0:T(8,128)S(1)}, f32[64,3328]{1,0:T(8,128)S(1)}, u32[]{:S(2)}, u32[]{:S(2)}) %collective-permute-start.2) | collective-permute-done | bytes 852000 | tf_op jit(solution)/shard_map/ppermute | solution.py:45
  191.3 0.1 fusion.2
  191.4 1.8 collective-permute-done.4
  193.3 1.0 pad_maximum_fusion
  (7 shorter events, 0.2 us)
Async XLA Ops:
  6.5 50.8 %all-gather.2.cloned.1.call-start = ((), (), s32[]{:S(2)}) async-start(), calls=%async_computation | async-start | bytes 2621440 | tf_op jit(solution)/shard_map/all_gather | solution.py:27
  105.2 11.3 %collective-permute-start = (f32[2,128,2,3328]{3,2,1,0:T(2,128)}, f32[2,128,2,3328]{3,2,1,0:T(2,128)}, u32[]{:S(2)}, u32[]{:S(2)}) collective-permute-start(f32[2,128,2,3328]{3,2,1,0:T(2,128)} %dynamic-slice_bitcast_fusion), channel_id=1, source_target_pairs={{0,4},{4,0},{8,12},{12,8},{1,5},{5,1},{9,13},{13,9},{2,6},{6,2},{1... | collective-permute-start | bytes 20447240 | tf_op jit(solution)/shard_map/ppermute | solution.py:37
  129.5 39.6 %collective-permute-start.1 = (f32[64,2,3328]{2,0,1:T(8,128)}, f32[64,2,3328]{2,0,1:T(8,128)}, u32[]{:S(2)}, u32[]{:S(2)}) collective-permute-start(f32[64,2,3328]{2,0,1:T(8,128)} %bitcast.35), channel_id=1, source_target_pairs={{0,8},{4,12},{8,0},{12,4},{1,9},{5,13},{9,1},{13,5},{2,10},{6,14},... | collective-permute-start | bytes 5111816 | tf_op jit(solution)/shard_map/ppermute | solution.py:41
  133.9 35.2 %copy-start = (f32[1,64,2,3328]{3,2,1,0:T(2,128)S(1)}, f32[1,64,2,3328]{3,2,1,0:T(2,128)}, u32[]{:S(2)}) copy-start(f32[1,64,2,3328]{3,2,1,0:T(2,128)} %get-tuple-element.7) | copy-start | bytes 5111812
  134.0 39.4 %collective-permute-start.3 = (f32[2,64,3328]{2,1,0:T(8,128)S(1)}, f32[2,64,3328]{2,1,0:T(8,128)S(1)}, u32[]{:S(2)}, u32[]{:S(2)}) collective-permute-start(f32[2,64,3328]{2,1,0:T(8,128)S(1)} %bitcast.36), channel_id=1, source_target_pairs={{0,16},{16,0},{1,17},{17,1},{2,18},{18,2},{3,19},{19,3},{4,20},{20... | collective-permute-start | bytes 5111816 | tf_op jit(solution)/shard_map/ppermute | solution.py:45
  170.7 20.5 %collective-permute-start.2 = (f32[64,3328]{1,0:T(8,128)S(1)}, f32[64,3328]{1,0:T(8,128)S(1)}, u32[]{:S(2)}, u32[]{:S(2)}) collective-permute-start(f32[64,3328]{1,0:T(8,128)S(1)} %dynamic-slice_bitcast_fusion.2), channel_id=1, source_target_pairs={{0,16},{16,0},{1,17},{17,1},{2,18},{18,2},{3,19},{19,3},{4,20},{20... | collective-permute-start | bytes 2555912 | tf_op jit(solution)/shard_map/ppermute | solution.py:45
  173.6 19.6 %collective-permute-start.4 = (f32[64,3328]{1,0:T(8,128)S(1)}, f32[64,3328]{1,0:T(8,128)S(1)}, u32[]{:S(2)}, u32[]{:S(2)}) collective-permute-start(f32[64,3328]{1,0:T(8,128)S(1)} %dynamic-slice_bitcast_fusion.1), channel_id=1, source_target_pairs={{0,8},{4,12},{8,0},{12,4},{1,9},{5,13},{9,1},{13,5},{2,10},{6,14},... | collective-permute-start | bytes 2555912 | tf_op jit(solution)/shard_map/ppermute | solution.py:41
Sparse Core Ops, SparseCore 0:
  8.9 48.3 all-gather.1

commit v2 on v1

v2 whole, which is shorter than its diff:
```python
import jax
import jax.numpy as jnp
from jax import lax
from jax.sharding import PartitionSpec as P


def ring_reduce_scatter(x, dim, size, index, shift):
    if size == 1:
        return lax.index_in_dim(x, 0, dim, keepdims=False)
    buf = lax.dynamic_index_in_dim(x, (index - 1) % size, dim, keepdims=False)
    for step in range(size - 1):
        received = shift(buf)
        chunk = (index - step - 2) % size
        buf = received + lax.dynamic_index_in_dim(x, chunk, dim, keepdims=False)
    return buf


def gather_tokens(tokens, n_col, col):
    received = [tokens]
    for steps in range(1, n_col):
        pairs = [(q, (q + steps) % n_col) for q in range(n_col)]
        received.append(lax.ppermute(tokens, "col", pairs))
    stacked = jnp.stack(received)
    order = (col - jnp.arange(n_col)) % n_col
    gathered = jnp.take(stacked, order, axis=0)
    return gathered.reshape(n_col * tokens.shape[0], tokens.shape[1])


def local(tokens, weight):
    n_row = lax.axis_size("row")
    n_depth = lax.axis_size("depth")
    n_col = lax.axis_size("col")
    row = lax.axis_index("row")
    depth = lax.axis_index("depth")
    col = lax.axis_index("col")
    core = row % 2
    hi = row // 2
    n_hi = n_row // 2

    gathered = gather_tokens(tokens, n_col, col)
    total = gathered.shape[0]
    width = weight.shape[1]
    block = total // n_row
    part = width // n_depth
    half = block // 2
    chunks = 2 if part % 256 == 0 else 1
    piece = part // chunks

    by_block = gathered.reshape(n_hi, 2, block, gathered.shape[1])
    own_rows = lax.dynamic_index_in_dim(by_block, core, 1, keepdims=False).reshape(n_hi * block, -1)
    other_rows = lax.dynamic_index_in_dim(by_block, 1 - core, 1, keepdims=False).reshape(n_hi * block, -1)

    partner = [(q, q ^ 1) for q in range(n_row)]

    def shift_hi(value):
        pairs = [(h * 2 + c, ((h + 1) % n_hi) * 2 + c) for h in range(n_hi) for c in range(2)]
        return lax.ppermute(value, "row", pairs)

    def shift_depth(value):
        pairs = [(q, (q + 1) % n_depth) for q in range(n_depth)]
        return lax.ppermute(value, "depth", pairs)

    def columns(d, q):
        start = d * part + q * piece
        return weight[:, start:start + piece]

    firsts, seconds = [], []
    for q in range(chunks):
        sent = [jnp.dot(other_rows, columns(d, q), preferred_element_type=jnp.float32) for d in range(n_depth)]
        arrived = lax.ppermute(sent, "row", partner)
        kept = [jnp.dot(own_rows, columns(d, q), preferred_element_type=jnp.float32) for d in range(n_depth)]
        summed = jnp.stack([(k + a).reshape(n_hi, block, piece) for k, a in zip(kept, arrived)])
        first = summed[:, :, :half]
        second = summed[:, :, half:]
        first = ring_reduce_scatter(first, 1, n_hi, hi, shift_hi)
        first = ring_reduce_scatter(first, 0, n_depth, depth, shift_depth)
        second = ring_reduce_scatter(second, 0, n_depth, depth, shift_depth)
        second = ring_reduce_scatter(second, 0, n_hi, hi, shift_hi)
        firsts.append(first)
        seconds.append(second)
    shares = jnp.concatenate(
        [jnp.concatenate(firsts, axis=1), jnp.concatenate(seconds, axis=1)], axis=0
    )
    return shares.astype(jnp.bfloat16).reshape(block, 1, part)


def solution(mesh):
    in_specs = (P("col", ("depth", "row")), P(("depth", "row"), "col"))
    out_specs = P("row", "col", "depth")
    return jax.shard_map(local, mesh=mesh, in_specs=in_specs, out_specs=out_specs, check_vma=False)
```

time: 202 us -> 149 us (0.74)
  local copies, waits for them, and re-layouts: 33.4 us -> 4.19 us
  waiting for transfers between devices: 116 us -> 91.4 us
  between operations: 13.5 us -> 0.26 us
  starting transfers between devices: 5.02 us -> 17.9 us
  matrix products: 22.8 us -> 29.5 us
  other arithmetic: 10.8 us -> 5.7 us
    all_gather x1 -> x0, waiting for transfers between devices: 50 us -> none  [local(): gathered = lax.all_gather(tokens, 'col', axis=0, tiled=True)]
    ppermute x1 -> x7, waiting for transfers between devices: 11.2 us -> 43.9 us  [the longest x3 43.9 us: gather_tokens(): received.append(lax.ppermute(tokens, 'col', pairs))]
    reshape x1 -> x0, local copies, waits for them, and re-layouts: 17 us -> none  [local(): product = product.reshape(n_hi, 2, block, n_depth, part)]
    ppermute x2 -> x4, waiting for transfers between devices: 35.3 us -> 24.1 us  [shift_hi(): return lax.ppermute(value, 'row', pairs)]
    squeeze x1 -> x0, local copies, waits for them, and re-layouts: 8.08 us -> none  [local(): send = lax.dynamic_index_in_dim(product, 1 - core, 1, keepdims=False)]
    add x1 -> x0, other arithmetic: 7.81 us -> none  [local(): summed = keep + lax.ppermute(send, 'row', partner)]
    ppermute x1 -> x7, starting transfers between devices: 0.01 us -> 7.29 us  [the longest x3 6.09 us: gather_tokens(): received.append(lax.ppermute(tokens, 'col', pairs))]
    dot_general x1 -> x8, matrix products: 22.8 us -> 29.5 us  [the longest x4 16.2 us: local(): jnp.dot(other_rows, columns(d, q), preferred_element_type=jnp.float32)]
  transfers between devices with their start and end apart: 6 -> 15, of which waited for: 6 -> 7; matrix products, arithmetic and copies ran while one was open for 3% -> 17% of each run, Pallas kernels for 0% -> 0%
where the time goes in v2:
time: 149 us
  waiting for transfers between devices  91.4 us (61%)
  matrix products  29.5 us (20%)
  starting transfers between devices  17.9 us (12%)
  other arithmetic  5.7 us (4%)
  local copies, waits for them, and re-layouts  4.19 us (3%)
    ppermute x3, waiting for transfers between devices, gather_tokens(): received.append(lax.ppermute(tokens, 'col', pairs))  43.9 us
    ppermute x4, waiting for transfers between devices, shift_hi(): return lax.ppermute(value, 'row', pairs)  24.1 us
    ppermute x4, waiting for transfers between devices, shift_depth(): return lax.ppermute(value, 'depth', pairs)  23.3 us
    dot_general x4, matrix products, local(): jnp.dot(other_rows, columns(d, q), preferred_element_type=jnp.float32)  16.2 us
    dot_general x4, matrix products, local(): jnp.dot(own_rows, columns(d, q), preferred_element_type=jnp.float32)  13.3 us
    ppermute x3, starting transfers between devices, gather_tokens(): received.append(lax.ppermute(tokens, 'col', pairs))  6.09 us
    ppermute x4, starting transfers between devices, shift_depth(): return lax.ppermute(value, 'depth', pairs)  5.31 us
    ppermute x4, starting transfers between devices, shift_hi(): return lax.ppermute(value, 'row', pairs)  5.27 us
  transfers between devices with their start and end apart: 15, of which 7 were waited for; matrix products, arithmetic and copies ran while one was open for 17% of the time, Pallas kernels for 0%

profile of v2, /device:TPU:0, one launch (start us, length us, event | category | flops | bytes accessed | tf_op | source)
XLA Modules:
  0.0 148.9 jit_solution(18164211101090365817)
XLA Ops:
  0.0 5.1 %collective-permute-start.2 = (bf16[128,2048]{1,0:T(8,128)(2,1)}, bf16[128,2048]{1,0:T(8,128)(2,1)S(1)}, u32[]{:S(2)}, u32[]{:S(2)}) collective-permute-start(bf16[128,2048]{1,0:T(8,128)(2,1)} %param.2), channel_id=1, source_target_pairs={{0,3},{1,0},{2,1},{3,2},{4,7},{5,4},{6,5},{7,6},{8,11},{9,8},{10,9... | collective-permute-start | bytes 1572872 | tf_op jit(solution)/shard_map/ppermute | solution.py:22
  6.1 11.6 %collective-permute-done.2 = bf16[128,2048]{1,0:T(8,128)(2,1)S(1)} collective-permute-done((bf16[128,2048]{1,0:T(8,128)(2,1)}, bf16[128,2048]{1,0:T(8,128)(2,1)S(1)}, u32[]{:S(2)}, u32[]{:S(2)}) %collective-permute-start.2) | collective-permute-done | bytes 524320 | tf_op jit(solution)/shard_map/ppermute | solution.py:22
  17.8 32.3 %collective-permute-done.1 = bf16[128,2048]{1,0:T(8,128)(2,1)S(1)} collective-permute-done((bf16[128,2048]{1,0:T(8,128)(2,1)}, bf16[128,2048]{1,0:T(8,128)(2,1)S(1)}, u32[]{:S(2)}, u32[]{:S(2)}) %collective-permute-start.1) | collective-permute-done | bytes 524320 | tf_op jit(solution)/shard_map/ppermute | solution.py:22
  52.3 2.0 %gather_fusion = bf16[4,128,2048]{2,1,0:T(8,128)(2,1)} fusion(bf16[4,128,2048]{2,1,0:T(8,128)(2,1)S(1)} %pad_maximum_fusion, s32[1024]{0:T(1024)S(1)} %pad_clamp_fusion), kind=kCustom, calls=%fused_computation | custom fusion | bytes 4194320 | tf_op jit(solution)/shard_map/jit(_take)/gather | solution.py:25
  54.4 1.9 %broadcast_select_fusion = bf16[2,2,128,2048]{3,2,1,0:T(8,128)(2,1)S(1)} fusion(bf16[2,2,128,2048]{3,2,1,0:T(8,128)(2,1)} %bitcast.81, pred[2,2]{1,0:T(4,128)(4,1)S(1)} %compare_and_fusion), kind=kLoop, calls=%fused_computation.26 | loop fusion | flops 1048576 | bytes 4194308 | tf_op jit(solution)/shard_map/jit(_take)/select_n | solution.py:25
  56.4 5.1 %fusion.4 = f32[256,1664]{1,0:T(8,128)S(1)} fusion(bf16[256,2048]{1,0:T(8,128)(2,1)S(1)} %bitcast.86, bf16[2048,6656]{1,0:T(8,128)(2,1)} %param.3), kind=kOutput, calls=%fused_computation.5 | convolution fusion | flops 1744830464 | bytes 9568256 | tf_op jit(solution)/shard_map/dot_general | solution.py:69
  61.6 5.7 %fusion = f32[256,1664]{1,0:T(8,128)S(1)} fusion(bf16[256,2048]{1,0:T(8,128)(2,1)S(1)} %bitcast.87, bf16[2048,6656]{1,0:T(8,128)(2,1)} %param.3), kind=kOutput, calls=%fused_computation.1 | convolution fusion | flops 1744830464 | bytes 9568256 | tf_op jit(solution)/shard_map/dot_general | solution.py:69
  68.9 2.1 %fusion.12 = f32[256,1664]{1,0:T(8,128)S(1)} fusion(bf16[256,2048]{1,0:T(8,128)(2,1)S(1)} %bitcast.88, bf16[2048,6656]{1,0:T(8,128)(2,1)S(1)} %copy-done.1), kind=kOutput, calls=%fused_computation.13 | convolution fusion | flops 1744830464 | bytes 9568256 | tf_op jit(solution)/shard_map/dot_general | solution.py:69
  71.0 3.2 %fusion.8 = f32[256,1664]{1,0:T(8,128)} fusion(bf16[256,2048]{1,0:T(8,128)(2,1)S(1)} %bitcast.89, bf16[2048,6656]{1,0:T(8,128)(2,1)S(1)} %copy-done.1), kind=kOutput, calls=%fused_computation.9 | convolution fusion | flops 1744830464 | bytes 9568256 | tf_op jit(solution)/shard_map/dot_general | solution.py:69
  74.8 2.1 %fusion.22 = f32[256,1664]{1,0:T(8,128)S(1)} fusion(f32[256,1664]{1,0:T(8,128)S(1)} %collective-permute-done.7, bf16[256,2048]{1,0:T(8,128)(2,1)S(1)} %bitcast.82, bf16[2048,6656]{1,0:T(8,128)(2,1)S(1)} %copy-done.1), kind=kOutput, calls=%fused_computation.23 | convolution fusion | flops 1745256448 | bytes 11272192 | tf_op jit(solution)/shard_map/dot_general | solution.py:71
  76.8 2.1 %fusion.25 = f32[256,1664]{1,0:T(8,128)S(1)} fusion(f32[256,1664]{1,0:T(8,128)S(1)} %collective-permute-done.8, bf16[256,2048]{1,0:T(8,128)(2,1)S(1)} %bitcast.83, bf16[2048,6656]{1,0:T(8,128)(2,1)S(1)} %copy-done.1), kind=kOutput, calls=%fused_computation.24 | convolution fusion | flops 1745256448 | bytes 11272192 | tf_op jit(solution)/shard_map/dot_general | solution.py:71
  79.1 1.6 %collective-permute-start.13 = (f32[2,64,1664]{2,1,0:T(8,128)S(1)}, f32[2,64,1664]{2,1,0:T(8,128)S(1)}, u32[]{:S(2)}, u32[]{:S(2)}) collective-permute-start(f32[2,64,1664]{2,1,0:T(8,128)S(1)} %fusion.39), channel_id=1, source_target_pairs={{0,16},{16,0},{1,17},{17,1},{2,18},{18,2},{3,19},{19,3},{4,20},{20... | collective-permute-start | bytes 2555912 | tf_op jit(solution)/shard_map/ppermute | solution.py:61
  80.8 3.7 %fusion.16 = f32[256,1664]{1,0:T(8,128)S(1)} fusion(f32[256,1664]{1,0:T(8,128)} %collective-permute-done.3, bf16[256,2048]{1,0:T(8,128)(2,1)S(1)} %bitcast.84, bf16[2048,6656]{1,0:T(8,128)(2,1)S(1)} %copy-done.1), kind=kOutput, calls=%fused_computation.21 | convolution fusion | flops 1745256448 | bytes 11272192 | tf_op jit(solution)/shard_map/dot_general | solution.py:71
  84.5 5.5 %fusion.19 = f32[256,1664]{1,0:T(8,128)S(1)} fusion(f32[256,1664]{1,0:T(8,128)} %collective-permute-done.4, bf16[256,2048]{1,0:T(8,128)(2,1)S(1)} %bitcast.85, bf16[2048,6656]{1,0:T(8,128)(2,1)} %param.3), kind=kOutput, calls=%fused_computation.22 | convolution fusion | flops 1745256448 | bytes 11272192 | tf_op jit(solution)/shard_map/dot_general | solution.py:71
  90.8 1.6 %collective-permute-start.9 = (f32[2,64,1664]{2,1,0:T(8,128)S(1)}, f32[2,64,1664]{2,1,0:T(8,128)S(1)}, u32[]{:S(2)}, u32[]{:S(2)}) collective-permute-start(f32[2,64,1664]{2,1,0:T(8,128)S(1)} %dynamic-slice_bitcast_fusion), channel_id=1, source_target_pairs={{0,8},{4,12},{8,0},{12,4},{1,9},{5,13},{9,1},{13,5},{2,10},{6,14},... | collective-permute-start | bytes 2555912 | tf_op jit(solution)/shard_map/ppermute | solution.py:57
  93.2 7.8 %collective-permute-done.13 = f32[2,64,1664]{2,1,0:T(8,128)S(1)} collective-permute-done((f32[2,64,1664]{2,1,0:T(8,128)S(1)}, f32[2,64,1664]{2,1,0:T(8,128)S(1)}, u32[]{:S(2)}, u32[]{:S(2)}) %collective-permute-start.13) | collective-permute-done | bytes 852000 | tf_op jit(solution)/shard_map/ppermute | solution.py:61
  101.2 1.6 %collective-permute-start.14 = (f32[64,1664]{1,0:T(8,128)S(1)}, f32[64,1664]{1,0:T(8,128)S(1)}, u32[]{:S(2)}, u32[]{:S(2)}) collective-permute-start(f32[64,1664]{1,0:T(8,128)S(1)} %dynamic-slice_bitcast_fusion.2), channel_id=1, source_target_pairs={{0,8},{4,12},{8,0},{12,4},{1,9},{5,13},{9,1},{13,5},{2,10},{6,14},... | collective-permute-start | bytes 1277960 | tf_op jit(solution)/shard_map/ppermute | solution.py:57
  102.8 15.5 %collective-permute-done.11 = f32[2,64,1664]{2,1,0:T(8,128)S(1)} collective-permute-done((f32[2,64,1664]{2,1,0:T(8,128)S(1)}, f32[2,64,1664]{2,1,0:T(8,128)S(1)}, u32[]{:S(2)}, u32[]{:S(2)}) %collective-permute-start.11) | collective-permute-done | bytes 852000 | tf_op jit(solution)/shard_map/ppermute | solution.py:61
  118.5 1.6 %collective-permute-start.12 = (f32[64,1664]{1,0:T(8,128)S(1)}, f32[64,1664]{1,0:T(8,128)S(1)}, u32[]{:S(2)}, u32[]{:S(2)}) collective-permute-start(f32[64,1664]{1,0:T(8,128)S(1)} %dynamic-slice_bitcast_fusion.3), channel_id=1, source_target_pairs={{0,8},{4,12},{8,0},{12,4},{1,9},{5,13},{9,1},{13,5},{2,10},{6,14},... | collective-permute-start | bytes 1277960 | tf_op jit(solution)/shard_map/ppermute | solution.py:57
  120.2 1.6 %collective-permute-start.10 = (f32[64,1664]{1,0:T(8,128)S(1)}, f32[64,1664]{1,0:T(8,128)S(1)}, u32[]{:S(2)}, u32[]{:S(2)}) collective-permute-start(f32[64,1664]{1,0:T(8,128)S(1)} %dynamic-slice_bitcast_fusion.4), channel_id=1, source_target_pairs={{0,16},{16,0},{1,17},{17,1},{2,18},{18,2},{3,19},{19,3},{4,20},{20... | collective-permute-start | bytes 1277960 | tf_op jit(solution)/shard_map/ppermute | solution.py:61
  121.8 9.2 %collective-permute-done.5 = f32[2,64,1664]{2,1,0:T(8,128)S(1)} collective-permute-done((f32[2,64,1664]{2,1,0:T(8,128)S(1)}, f32[2,64,1664]{2,1,0:T(8,128)S(1)}, u32[]{:S(2)}, u32[]{:S(2)}) %collective-permute-start.5) | collective-permute-done | bytes 852000 | tf_op jit(solution)/shard_map/ppermute | solution.py:57
  131.1 1.6 %collective-permute-start.6 = (f32[64,1664]{1,0:T(8,128)S(1)}, f32[64,1664]{1,0:T(8,128)S(1)}, u32[]{:S(2)}, u32[]{:S(2)}) collective-permute-start(f32[64,1664]{1,0:T(8,128)S(1)} %dynamic-slice_bitcast_fusion.5), channel_id=1, source_target_pairs={{0,16},{16,0},{1,17},{17,1},{2,18},{18,2},{3,19},{19,3},{4,20},{20... | collective-permute-start | bytes 1277960 | tf_op jit(solution)/shard_map/ppermute | solution.py:61
  132.7 7.4 %collective-permute-done.14 = f32[64,1664]{1,0:T(8,128)S(1)} collective-permute-done((f32[64,1664]{1,0:T(8,128)S(1)}, f32[64,1664]{1,0:T(8,128)S(1)}, u32[]{:S(2)}, u32[]{:S(2)}) %collective-permute-start.14) | collective-permute-done | bytes 426016 | tf_op jit(solution)/shard_map/ppermute | solution.py:57
  140.1 7.6 %collective-permute-done.12 = f32[64,1664]{1,0:T(8,128)S(1)} collective-permute-done((f32[64,1664]{1,0:T(8,128)S(1)}, f32[64,1664]{1,0:T(8,128)S(1)}, u32[]{:S(2)}, u32[]{:S(2)}) %collective-permute-start.12) | collective-permute-done | bytes 426016 | tf_op jit(solution)/shard_map/ppermute | solution.py:57
  (46 shorter events, 9.4 us)
Async XLA Ops:
  0.0 17.7 %collective-permute-start.2 = (bf16[128,2048]{1,0:T(8,128)(2,1)}, bf16[128,2048]{1,0:T(8,128)(2,1)S(1)}, u32[]{:S(2)}, u32[]{:S(2)}) collective-permute-start(bf16[128,2048]{1,0:T(8,128)(2,1)} %param.2), channel_id=1, source_target_pairs={{0,3},{1,0},{2,1},{3,2},{4,7},{5,4},{6,5},{7,6},{8,11},{9,8},{10,9... | collective-permute-start | bytes 1572872 | tf_op jit(solution)/shard_map/ppermute | solution.py:22
  5.1 45.0 %collective-permute-start.1 = (bf16[128,2048]{1,0:T(8,128)(2,1)}, bf16[128,2048]{1,0:T(8,128)(2,1)S(1)}, u32[]{:S(2)}, u32[]{:S(2)}) collective-permute-start(bf16[128,2048]{1,0:T(8,128)(2,1)} %param.2), channel_id=1, source_target_pairs={{0,2},{1,3},{2,0},{3,1},{4,6},{5,7},{6,4},{7,5},{8,10},{9,11},{10,... | collective-permute-start | bytes 1572872 | tf_op jit(solution)/shard_map/ppermute | solution.py:22
  5.1 45.0 %collective-permute-start = (bf16[128,2048]{1,0:T(8,128)(2,1)}, bf16[128,2048]{1,0:T(8,128)(2,1)S(1)}, u32[]{:S(2)}, u32[]{:S(2)}) collective-permute-start(bf16[128,2048]{1,0:T(8,128)(2,1)} %param.2), channel_id=1, source_target_pairs={{0,1},{1,2},{2,3},{3,0},{4,5},{5,6},{6,7},{7,4},{8,9},{9,10},{10,1... | collective-permute-start | bytes 1572872 | tf_op jit(solution)/shard_map/ppermute | solution.py:22
  50.1 0.8 copy-start
  56.2 12.7 %copy-start.1 = (bf16[2048,6656]{1,0:T(8,128)(2,1)S(1)}, bf16[2048,6656]{1,0:T(8,128)(2,1)}, u32[]{:S(2)}) copy-start(bf16[2048,6656]{1,0:T(8,128)(2,1)} %param.3) | copy-start | bytes 81788928
  61.5 13.2 %collective-permute-start.7 = (f32[256,1664]{1,0:T(8,128)S(1)}, f32[256,1664]{1,0:T(8,128)S(1)}, u32[]{:S(2)}, u32[]{:S(2)}) collective-permute-start(f32[256,1664]{1,0:T(8,128)S(1)} %fusion.4), channel_id=1, source_target_pairs={{0,4},{4,0},{8,12},{12,8},{1,5},{5,1},{9,13},{13,9},{2,6},{6,2},{1... | collective-permute-start | bytes 5111816 | tf_op jit(solution)/shard_map/ppermute | solution.py:70
  67.4 9.5 %collective-permute-start.8 = (f32[256,1664]{1,0:T(8,128)S(1)}, f32[256,1664]{1,0:T(8,128)S(1)}, u32[]{:S(2)}, u32[]{:S(2)}) collective-permute-start(f32[256,1664]{1,0:T(8,128)S(1)} %fusion), channel_id=1, source_target_pairs={{0,4},{4,0},{8,12},{12,8},{1,5},{5,1},{9,13},{13,9},{2,6},{6,2},{1... | collective-permute-start | bytes 5111816 | tf_op jit(solution)/shard_map/ppermute | solution.py:70
  70.9 9.9 %collective-permute-start.3 = (f32[256,1664]{1,0:T(8,128)S(1)}, f32[256,1664]{1,0:T(8,128)}, u32[]{:S(2)}, u32[]{:S(2)}) collective-permute-start(f32[256,1664]{1,0:T(8,128)S(1)} %fusion.12), channel_id=1, source_target_pairs={{0,4},{4,0},{8,12},{12,8},{1,5},{5,1},{9,13},{13,9},{2,6},{6,2},{1... | collective-permute-start | bytes 5111816 | tf_op jit(solution)/shard_map/ppermute | solution.py:70
  74.3 10.3 %collective-permute-start.4 = (f32[256,1664]{1,0:T(8,128)}, f32[256,1664]{1,0:T(8,128)}, u32[]{:S(2)}, u32[]{:S(2)}) collective-permute-start(f32[256,1664]{1,0:T(8,128)} %fusion.8), channel_id=1, source_target_pairs={{0,4},{4,0},{8,12},{12,8},{1,5},{5,1},{9,13},{13,9},{2,6},{6,2},{1... | collective-permute-start | bytes 5111816 | tf_op jit(solution)/shard_map/ppermute | solution.py:70
  79.1 21.9 %collective-permute-start.13 = (f32[2,64,1664]{2,1,0:T(8,128)S(1)}, f32[2,64,1664]{2,1,0:T(8,128)S(1)}, u32[]{:S(2)}, u32[]{:S(2)}) collective-permute-start(f32[2,64,1664]{2,1,0:T(8,128)S(1)} %fusion.39), channel_id=1, source_target_pairs={{0,16},{16,0},{1,17},{17,1},{2,18},{18,2},{3,19},{19,3},{4,20},{20... | collective-permute-start | bytes 2555912 | tf_op jit(solution)/shard_map/ppermute | solution.py:61
  90.2 28.1 %collective-permute-start.11 = (f32[2,64,1664]{2,1,0:T(8,128)S(1)}, f32[2,64,1664]{2,1,0:T(8,128)S(1)}, u32[]{:S(2)}, u32[]{:S(2)}) collective-permute-start(f32[2,64,1664]{2,1,0:T(8,128)S(1)} %fusion.34), channel_id=1, source_target_pairs={{0,16},{16,0},{1,17},{17,1},{2,18},{18,2},{3,19},{19,3},{4,20},{20... | collective-permute-start | bytes 2555912 | tf_op jit(solution)/shard_map/ppermute | solution.py:61
  90.8 29.3 %collective-permute-start.9 = (f32[2,64,1664]{2,1,0:T(8,128)S(1)}, f32[2,64,1664]{2,1,0:T(8,128)S(1)}, u32[]{:S(2)}, u32[]{:S(2)}) collective-permute-start(f32[2,64,1664]{2,1,0:T(8,128)S(1)} %dynamic-slice_bitcast_fusion), channel_id=1, source_target_pairs={{0,8},{4,12},{8,0},{12,4},{1,9},{5,13},{9,1},{13,5},{2,10},{6,14},... | collective-permute-start | bytes 2555912 | tf_op jit(solution)/shard_map/ppermute | solution.py:57
  92.6 38.4 %collective-permute-start.5 = (f32[2,64,1664]{2,1,0:T(8,128)S(1)}, f32[2,64,1664]{2,1,0:T(8,128)S(1)}, u32[]{:S(2)}, u32[]{:S(2)}) collective-permute-start(f32[2,64,1664]{2,1,0:T(8,128)S(1)} %dynamic-slice_bitcast_fusion.1), channel_id=1, source_target_pairs={{0,8},{4,12},{8,0},{12,4},{1,9},{5,13},{9,1},{13,5},{2,10},{6,14},... | collective-permute-start | bytes 2555912 | tf_op jit(solution)/shard_map/ppermute | solution.py:57
  101.2 38.9 %collective-permute-start.14 = (f32[64,1664]{1,0:T(8,128)S(1)}, f32[64,1664]{1,0:T(8,128)S(1)}, u32[]{:S(2)}, u32[]{:S(2)}) collective-permute-start(f32[64,1664]{1,0:T(8,128)S(1)} %dynamic-slice_bitcast_fusion.2), channel_id=1, source_target_pairs={{0,8},{4,12},{8,0},{12,4},{1,9},{5,13},{9,1},{13,5},{2,10},{6,14},... | collective-permute-start | bytes 1277960 | tf_op jit(solution)/shard_map/ppermute | solution.py:57
  118.5 29.2 %collective-permute-start.12 = (f32[64,1664]{1,0:T(8,128)S(1)}, f32[64,1664]{1,0:T(8,128)S(1)}, u32[]{:S(2)}, u32[]{:S(2)}) collective-permute-start(f32[64,1664]{1,0:T(8,128)S(1)} %dynamic-slice_bitcast_fusion.3), channel_id=1, source_target_pairs={{0,8},{4,12},{8,0},{12,4},{1,9},{5,13},{9,1},{13,5},{2,10},{6,14},... | collective-permute-start | bytes 1277960 | tf_op jit(solution)/shard_map/ppermute | solution.py:57
  120.2 27.5 %collective-permute-start.10 = (f32[64,1664]{1,0:T(8,128)S(1)}, f32[64,1664]{1,0:T(8,128)S(1)}, u32[]{:S(2)}, u32[]{:S(2)}) collective-permute-start(f32[64,1664]{1,0:T(8,128)S(1)} %dynamic-slice_bitcast_fusion.4), channel_id=1, source_target_pairs={{0,16},{16,0},{1,17},{17,1},{2,18},{18,2},{3,19},{19,3},{4,20},{20... | collective-permute-start | bytes 1277960 | tf_op jit(solution)/shard_map/ppermute | solution.py:61
  131.1 16.8 %collective-permute-start.6 = (f32[64,1664]{1,0:T(8,128)S(1)}, f32[64,1664]{1,0:T(8,128)S(1)}, u32[]{:S(2)}, u32[]{:S(2)}) collective-permute-start(f32[64,1664]{1,0:T(8,128)S(1)} %dynamic-slice_bitcast_fusion.5), channel_id=1, source_target_pairs={{0,16},{16,0},{1,17},{17,1},{2,18},{18,2},{3,19},{19,3},{4,20},{20... | collective-permute-start | bytes 1277960 | tf_op jit(solution)/shard_map/ppermute | solution.py:61

commit v3 on v2

--- a/solution.py
+++ b/solution.py
@@ -16,13 +16,17 @@
 
 
 def gather_tokens(tokens, n_col, col):
-    received = [tokens]
-    for steps in range(1, n_col):
-        pairs = [(q, (q + steps) % n_col) for q in range(n_col)]
-        received.append(lax.ppermute(tokens, "col", pairs))
-    stacked = jnp.stack(received)
-    order = (col - jnp.arange(n_col)) % n_col
-    gathered = jnp.take(stacked, order, axis=0)
+    rightward = [(q, q + 1) for q in range(n_col - 1)]
+    leftward = [(q + 1, q) for q in range(n_col - 1)]
+    from_left, from_right = [], []
+    going_right = going_left = tokens
+    for _ in range(1, n_col):
+        going_right = lax.ppermute(going_right, "col", rightward)
+        going_left = lax.ppermute(going_left, "col", leftward)
+        from_left.append(going_right)
+        from_right.append(going_left)
+    line = jnp.stack(from_left[::-1] + [tokens] + from_right)
+    gathered = lax.dynamic_slice_in_dim(line, n_col - 1 - col, n_col, 0)
     return gathered.reshape(n_col * tokens.shape[0], tokens.shape[1])
 
 
@@ -43,8 +47,9 @@
     block = total // n_row
     part = width // n_depth
     half = block // 2
-    chunks = 2 if part % 256 == 0 else 1
-    piece = part // chunks
+    lanes = part // 128 if part % 128 == 0 else 1
+    chunks = min(4, lanes)
+    bounds = [(lanes * q // chunks) * (part // lanes) for q in range(chunks + 1)]
 
     by_block = gathered.reshape(n_hi, 2, block, gathered.shape[1])
     own_rows = lax.dynamic_index_in_dim(by_block, core, 1, keepdims=False).reshape(n_hi * block, -1)
@@ -61,15 +66,14 @@
         return lax.ppermute(value, "depth", pairs)
 
     def columns(d, q):
-        start = d * part + q * piece
-        return weight[:, start:start + piece]
+        return weight[:, d * part + bounds[q]:d * part + bounds[q + 1]]
 
     firsts, seconds = [], []
     for q in range(chunks):
         sent = [jnp.dot(other_rows, columns(d, q), preferred_element_type=jnp.float32) for d in range(n_depth)]
         arrived = lax.ppermute(sent, "row", partner)
         kept = [jnp.dot(own_rows, columns(d, q), preferred_element_type=jnp.float32) for d in range(n_depth)]
-        summed = jnp.stack([(k + a).reshape(n_hi, block, piece) for k, a in zip(kept, arrived)])
+        summed = jnp.stack([(k + a).reshape(n_hi, block, -1) for k, a in zip(kept, arrived)])
         first = summed[:, :, :half]
         second = summed[:, :, half:]
         first = ring_reduce_scatter(first, 1, n_hi, hi, shift_hi)

time: 149 us -> 135 us (0.906)
  waiting for transfers between devices: 91.4 us -> 68.9 us
  starting transfers between devices: 17.9 us -> 38.5 us
  matrix products: 29.5 us -> 22.8 us
  other arithmetic: 5.7 us -> 2.43 us
  local copies, waits for them, and re-layouts: 4.19 us -> 0.98 us
    ppermute x3 -> x6, waiting for transfers between devices: 43.9 us -> 31.1 us  [the longest x3 27.1 us: gather_tokens(): going_right = lax.ppermute(going_right, 'col', rightward)]
    ppermute x3 -> x6, starting transfers between devices: 6.09 us -> 17.7 us  [the longest x3 13.8 us: gather_tokens(): going_right = lax.ppermute(going_right, 'col', rightward)]
    ppermute x4 -> x8, waiting for transfers between devices: 23.3 us -> 17.4 us  [shift_depth(): return lax.ppermute(value, 'depth', pairs)]
    ppermute x4 -> x8, starting transfers between devices: 5.31 us -> 10.3 us  [shift_depth(): return lax.ppermute(value, 'depth', pairs)]
    ppermute x4 -> x8, waiting for transfers between devices: 24.1 us -> 19.2 us  [shift_hi(): return lax.ppermute(value, 'row', pairs)]
    dot_general x4 -> x8, matrix products: 13.3 us -> 8.9 us  [local(): jnp.dot(own_rows, columns(d, q), preferred_element_type=jnp.float32)]
    ppermute x4 -> x8, starting transfers between devices: 5.27 us -> 8.59 us  [shift_hi(): return lax.ppermute(value, 'row', pairs)]
    dot_general x4 -> x8, matrix products: 16.2 us -> 13.9 us  [local(): jnp.dot(other_rows, columns(d, q), preferred_element_type=jnp.float32)]
  transfers between devices with their start and end apart: 15 -> 30, of which waited for: 7 -> 15; matrix products, arithmetic and copies ran while one was open for 17% -> 10% of each run, Pallas kernels for 0% -> 0%
where the time goes in v3:
time: 135 us
  waiting for transfers between devices  68.9 us (51%)
  starting transfers between devices  38.5 us (29%)
  matrix products  22.8 us (17%)
  other arithmetic  2.43 us (2%)
    ppermute x3, waiting for transfers between devices, gather_tokens(): going_right = lax.ppermute(going_right, 'col', rightward)  27.1 us
    ppermute x8, waiting for transfers between devices, shift_hi(): return lax.ppermute(value, 'row', pairs)  19.2 us
    ppermute x8, waiting for transfers between devices, shift_depth(): return lax.ppermute(value, 'depth', pairs)  17.4 us
    dot_general x8, matrix products, local(): jnp.dot(other_rows, columns(d, q), preferred_element_type=jnp.float32)  13.9 us
    ppermute x3, starting transfers between devices, gather_tokens(): going_right = lax.ppermute(going_right, 'col', rightward)  13.8 us
    ppermute x8, starting transfers between devices, shift_depth(): return lax.ppermute(value, 'depth', pairs)  10.3 us
    dot_general x8, matrix products, local(): jnp.dot(own_rows, columns(d, q), preferred_element_type=jnp.float32)  8.9 us
    ppermute x8, starting transfers between devices, shift_hi(): return lax.ppermute(value, 'row', pairs)  8.59 us
  transfers between devices with their start and end apart: 30, of which 15 were waited for; matrix products, arithmetic and copies ran while one was open for 10% of the time, Pallas kernels for 0%

profile of v3, /device:TPU:0, one launch (start us, length us, event | category | flops | bytes accessed | tf_op | source)
XLA Modules:
  0.0 134.5 jit_solution(16401803913192193211)
XLA Ops:
  0.0 5.1 %collective-permute-start = (bf16[128,2048]{1,0:T(8,128)(2,1)}, bf16[128,2048]{1,0:T(8,128)(2,1)S(1)}, u32[]{:S(2)}, u32[]{:S(2)}) collective-permute-start(bf16[128,2048]{1,0:T(8,128)(2,1)} %param.2), channel_id=1, source_target_pairs={{0,1},{1,2},{2,3},{4,5},{5,6},{6,7},{8,9},{9,10},{10,11},{12,13},{... | collective-permute-start | bytes 1572872 | tf_op jit(solution)/shard_map/ppermute | solution.py:24
  6.4 10.1 %collective-permute-done = bf16[128,2048]{1,0:T(8,128)(2,1)S(1)} collective-permute-done((bf16[128,2048]{1,0:T(8,128)(2,1)}, bf16[128,2048]{1,0:T(8,128)(2,1)S(1)}, u32[]{:S(2)}, u32[]{:S(2)}) %collective-permute-start) | collective-permute-done | bytes 524320 | tf_op jit(solution)/shard_map/ppermute | solution.py:24
  16.6 4.3 %collective-permute-start.1 = (bf16[128,2048]{1,0:T(8,128)(2,1)S(1)}, bf16[128,2048]{1,0:T(8,128)(2,1)S(1)}, u32[]{:S(2)}, u32[]{:S(2)}) collective-permute-start(bf16[128,2048]{1,0:T(8,128)(2,1)S(1)} %collective-permute-done), channel_id=1, source_target_pairs={{0,1},{1,2},{2,3},{4,5},{5,6},{6,7},{8,9},{9,10},{10,11},{12,13},{... | collective-permute-start | bytes 1572872 | tf_op jit(solution)/shard_map/ppermute | solution.py:24
  22.2 9.0 %collective-permute-done.1 = bf16[128,2048]{1,0:T(8,128)(2,1)S(1)} collective-permute-done((bf16[128,2048]{1,0:T(8,128)(2,1)S(1)}, bf16[128,2048]{1,0:T(8,128)(2,1)S(1)}, u32[]{:S(2)}, u32[]{:S(2)}) %collective-permute-start.1) | collective-permute-done | bytes 524320 | tf_op jit(solution)/shard_map/ppermute | solution.py:24
  31.2 4.4 %collective-permute-start.2 = (bf16[128,2048]{1,0:T(8,128)(2,1)S(1)}, bf16[128,2048]{1,0:T(8,128)(2,1)S(1)}, u32[]{:S(2)}, u32[]{:S(2)}) collective-permute-start(bf16[128,2048]{1,0:T(8,128)(2,1)S(1)} %collective-permute-done.1), channel_id=1, source_target_pairs={{0,1},{1,2},{2,3},{4,5},{5,6},{6,7},{8,9},{9,10},{10,11},{12,13},{... | collective-permute-start | bytes 1572872 | tf_op jit(solution)/shard_map/ppermute | solution.py:24
  37.0 8.0 %collective-permute-done.2 = bf16[128,2048]{1,0:T(8,128)(2,1)S(1)} collective-permute-done((bf16[128,2048]{1,0:T(8,128)(2,1)S(1)}, bf16[128,2048]{1,0:T(8,128)(2,1)S(1)}, u32[]{:S(2)}, u32[]{:S(2)}) %collective-permute-start.2) | collective-permute-done | bytes 524320 | tf_op jit(solution)/shard_map/ppermute | solution.py:24
  45.3 4.0 %collective-permute-done.5 = bf16[128,2048]{1,0:T(8,128)(2,1)S(1)} collective-permute-done((bf16[128,2048]{1,0:T(8,128)(2,1)S(1)}, bf16[128,2048]{1,0:T(8,128)(2,1)S(1)}, u32[]{:S(2)}, u32[]{:S(2)}) %collective-permute-start.5) | collective-permute-done | bytes 524320 | tf_op jit(solution)/shard_map/ppermute | solution.py:25
  49.7 3.6 %fusion.24 = f32[256,768]{1,0:T(8,128)S(1)} fusion(bf16[256,2048]{1,0:T(8,128)(2,1)S(1)} %bitcast.166, bf16[2048,6656]{1,0:T(8,128)(2,1)} %param.3), kind=kOutput, calls=%fused_computation.24 | convolution fusion | flops 805306368 | bytes 4980736 | tf_op jit(solution)/shard_map/dot_general | solution.py:73
  53.3 3.3 %fusion.28 = f32[256,768]{1,0:T(8,128)S(1)} fusion(bf16[256,2048]{1,0:T(8,128)(2,1)S(1)} %bitcast.167, bf16[2048,6656]{1,0:T(8,128)(2,1)} %param.3), kind=kOutput, calls=%fused_computation.28 | convolution fusion | flops 805306368 | bytes 4980736 | tf_op jit(solution)/shard_map/dot_general | solution.py:73
  69.8 1.6 %collective-permute-start.8 = (f32[2,64,768]{2,1,0:T(8,128)S(1)}, f32[2,64,768]{2,1,0:T(8,128)S(1)}, u32[]{:S(2)}, u32[]{:S(2)}) collective-permute-start(f32[2,64,768]{2,1,0:T(8,128)S(1)} %dynamic-slice_bitcast_fusion.3), channel_id=1, source_target_pairs={{0,8},{4,12},{8,0},{12,4},{1,9},{5,13},{9,1},{13,5},{2,10},{6,14},... | collective-permute-start | bytes 1179656 | tf_op jit(solution)/shard_map/ppermute | solution.py:62
  74.7 1.6 %collective-permute-start.22 = (f32[2,64,768]{2,1,0:T(8,128)S(1)}, f32[2,64,768]{2,1,0:T(8,128)S(1)}, u32[]{:S(2)}, u32[]{:S(2)}) collective-permute-start(f32[2,64,768]{2,1,0:T(8,128)S(1)} %fusion.74), channel_id=1, source_target_pairs={{0,16},{16,0},{1,17},{17,1},{2,18},{18,2},{3,19},{19,3},{4,20},{20... | collective-permute-start | bytes 1179656 | tf_op jit(solution)/shard_map/ppermute | solution.py:66
  81.1 1.6 %collective-permute-start.12 = (f32[2,64,896]{2,1,0:T(8,128)S(1)}, f32[2,64,896]{2,1,0:T(8,128)S(1)}, u32[]{:S(2)}, u32[]{:S(2)}) collective-permute-start(f32[2,64,896]{2,1,0:T(8,128)S(1)} %dynamic-slice_bitcast_fusion.1), channel_id=1, source_target_pairs={{0,8},{4,12},{8,0},{12,4},{1,9},{5,13},{9,1},{13,5},{2,10},{6,14},... | collective-permute-start | bytes 1376264 | tf_op jit(solution)/shard_map/ppermute | solution.py:62
  83.4 6.9 %collective-permute-done.16 = f32[2,64,768]{2,1,0:T(8,128)S(1)} collective-permute-done((f32[2,64,768]{2,1,0:T(8,128)S(1)}, f32[2,64,768]{2,1,0:T(8,128)S(1)}, u32[]{:S(2)}, u32[]{:S(2)}) %collective-permute-start.16) | collective-permute-done | bytes 393248 | tf_op jit(solution)/shard_map/ppermute | solution.py:62
  90.3 1.5 %collective-permute-start.24 = (f32[2,64,896]{2,1,0:T(8,128)S(1)}, f32[2,64,896]{2,1,0:T(8,128)S(1)}, u32[]{:S(2)}, u32[]{:S(2)}) collective-permute-start(f32[2,64,896]{2,1,0:T(8,128)S(1)} %fusion.64), channel_id=1, source_target_pairs={{0,16},{16,0},{1,17},{17,1},{2,18},{18,2},{3,19},{19,3},{4,20},{20... | collective-permute-start | bytes 1376264 | tf_op jit(solution)/shard_map/ppermute | solution.py:66
  92.6 2.6 %collective-permute-done.26 = f32[2,64,768]{2,1,0:T(8,128)S(1)} collective-permute-done((f32[2,64,768]{2,1,0:T(8,128)S(1)}, f32[2,64,768]{2,1,0:T(8,128)S(1)}, u32[]{:S(2)}, u32[]{:S(2)}) %collective-permute-start.26) | collective-permute-done | bytes 393248 | tf_op jit(solution)/shard_map/ppermute | solution.py:66
  95.2 1.5 %collective-permute-start.9 = (f32[64,768]{1,0:T(8,128)S(1)}, f32[64,768]{1,0:T(8,128)S(1)}, u32[]{:S(2)}, u32[]{:S(2)}) collective-permute-start(f32[64,768]{1,0:T(8,128)S(1)} %dynamic-slice_bitcast_fusion.11), channel_id=1, source_target_pairs={{0,16},{16,0},{1,17},{17,1},{2,18},{18,2},{3,19},{19,3},{4,20},{20... | collective-permute-start | bytes 589832 | tf_op jit(solution)/shard_map/ppermute | solution.py:66
  96.8 3.3 %collective-permute-done.12 = f32[2,64,896]{2,1,0:T(8,128)S(1)} collective-permute-done((f32[2,64,896]{2,1,0:T(8,128)S(1)}, f32[2,64,896]{2,1,0:T(8,128)S(1)}, u32[]{:S(2)}, u32[]{:S(2)}) %collective-permute-start.12) | collective-permute-done | bytes 458784 | tf_op jit(solution)/shard_map/ppermute | solution.py:62
  100.1 1.5 %collective-permute-start.17 = (f32[64,768]{1,0:T(8,128)S(1)}, f32[64,768]{1,0:T(8,128)S(1)}, u32[]{:S(2)}, u32[]{:S(2)}) collective-permute-start(f32[64,768]{1,0:T(8,128)S(1)} %dynamic-slice_bitcast_fusion.10), channel_id=1, source_target_pairs={{0,16},{16,0},{1,17},{17,1},{2,18},{18,2},{3,19},{19,3},{4,20},{20... | collective-permute-start | bytes 589832 | tf_op jit(solution)/shard_map/ppermute | solution.py:66
  101.7 7.7 %collective-permute-done.20 = f32[2,64,896]{2,1,0:T(8,128)S(1)} collective-permute-done((f32[2,64,896]{2,1,0:T(8,128)S(1)}, f32[2,64,896]{2,1,0:T(8,128)S(1)}, u32[]{:S(2)}, u32[]{:S(2)}) %collective-permute-start.20) | collective-permute-done | bytes 458784 | tf_op jit(solution)/shard_map/ppermute | solution.py:62
  111.7 3.2 %collective-permute-done.28 = f32[2,64,896]{2,1,0:T(8,128)S(1)} collective-permute-done((f32[2,64,896]{2,1,0:T(8,128)S(1)}, f32[2,64,896]{2,1,0:T(8,128)S(1)}, u32[]{:S(2)}, u32[]{:S(2)}) %collective-permute-start.28) | collective-permute-done | bytes 458784 | tf_op jit(solution)/shard_map/ppermute | solution.py:66
  116.5 2.5 %collective-permute-done.9 = f32[64,768]{1,0:T(8,128)S(1)} collective-permute-done((f32[64,768]{1,0:T(8,128)S(1)}, f32[64,768]{1,0:T(8,128)S(1)}, u32[]{:S(2)}, u32[]{:S(2)}) %collective-permute-start.9) | collective-permute-done | bytes 196640 | tf_op jit(solution)/shard_map/ppermute | solution.py:66
  120.6 2.7 %collective-permute-done.17 = f32[64,768]{1,0:T(8,128)S(1)} collective-permute-done((f32[64,768]{1,0:T(8,128)S(1)}, f32[64,768]{1,0:T(8,128)S(1)}, u32[]{:S(2)}, u32[]{:S(2)}) %collective-permute-start.17) | collective-permute-done | bytes 196640 | tf_op jit(solution)/shard_map/ppermute | solution.py:66
  125.5 2.7 %collective-permute-done.13 = f32[64,896]{1,0:T(8,128)S(1)} collective-permute-done((f32[64,896]{1,0:T(8,128)S(1)}, f32[64,896]{1,0:T(8,128)S(1)}, u32[]{:S(2)}, u32[]{:S(2)}) %collective-permute-start.13) | collective-permute-done | bytes 229408 | tf_op jit(solution)/shard_map/ppermute | solution.py:66
  128.2 3.7 %collective-permute-done.21 = f32[64,896]{1,0:T(8,128)S(1)} collective-permute-done((f32[64,896]{1,0:T(8,128)S(1)}, f32[64,896]{1,0:T(8,128)S(1)}, u32[]{:S(2)}, u32[]{:S(2)}) %collective-permute-start.21) | collective-permute-done | bytes 229408 | tf_op jit(solution)/shard_map/ppermute | solution.py:66
  (104 shorter events, 37.3 us)
Async XLA Ops:
  0.0 16.6 %collective-permute-start = (bf16[128,2048]{1,0:T(8,128)(2,1)}, bf16[128,2048]{1,0:T(8,128)(2,1)S(1)}, u32[]{:S(2)}, u32[]{:S(2)}) collective-permute-start(bf16[128,2048]{1,0:T(8,128)(2,1)} %param.2), channel_id=1, source_target_pairs={{0,1},{1,2},{2,3},{4,5},{5,6},{6,7},{8,9},{9,10},{10,11},{12,13},{... | collective-permute-start | bytes 1572872 | tf_op jit(solution)/shard_map/ppermute | solution.py:24
  5.1 15.8 %collective-permute-start.3 = (bf16[128,2048]{1,0:T(8,128)(2,1)}, bf16[128,2048]{1,0:T(8,128)(2,1)S(1)}, u32[]{:S(2)}, u32[]{:S(2)}) collective-permute-start(bf16[128,2048]{1,0:T(8,128)(2,1)} %param.2), channel_id=1, source_target_pairs={{1,0},{2,1},{3,2},{5,4},{6,5},{7,6},{9,8},{10,9},{11,10},{13,12},{... | collective-permute-start | bytes 1572872 | tf_op jit(solution)/shard_map/ppermute | solution.py:25
  16.6 14.6 %collective-permute-start.1 = (bf16[128,2048]{1,0:T(8,128)(2,1)S(1)}, bf16[128,2048]{1,0:T(8,128)(2,1)S(1)}, u32[]{:S(2)}, u32[]{:S(2)}) collective-permute-start(bf16[128,2048]{1,0:T(8,128)(2,1)S(1)} %collective-permute-done), channel_id=1, source_target_pairs={{0,1},{1,2},{2,3},{4,5},{5,6},{6,7},{8,9},{9,10},{10,11},{12,13},{... | collective-permute-start | bytes 1572872 | tf_op jit(solution)/shard_map/ppermute | solution.py:24
  20.9 14.8 %collective-permute-start.4 = (bf16[128,2048]{1,0:T(8,128)(2,1)S(1)}, bf16[128,2048]{1,0:T(8,128)(2,1)S(1)}, u32[]{:S(2)}, u32[]{:S(2)}) collective-permute-start(bf16[128,2048]{1,0:T(8,128)(2,1)S(1)} %collective-permute-done.3), channel_id=1, source_target_pairs={{1,0},{2,1},{3,2},{5,4},{6,5},{7,6},{9,8},{10,9},{11,10},{13,12},{... | collective-permute-start | bytes 1572872 | tf_op jit(solution)/shard_map/ppermute | solution.py:25
  31.2 13.8 %collective-permute-start.2 = (bf16[128,2048]{1,0:T(8,128)(2,1)S(1)}, bf16[128,2048]{1,0:T(8,128)(2,1)S(1)}, u32[]{:S(2)}, u32[]{:S(2)}) collective-permute-start(bf16[128,2048]{1,0:T(8,128)(2,1)S(1)} %collective-permute-done.1), channel_id=1, source_target_pairs={{0,1},{1,2},{2,3},{4,5},{5,6},{6,7},{8,9},{9,10},{10,11},{12,13},{... | collective-permute-start | bytes 1572872 | tf_op jit(solution)/shard_map/ppermute | solution.py:24
  35.7 13.6 %collective-permute-start.5 = (bf16[128,2048]{1,0:T(8,128)(2,1)S(1)}, bf16[128,2048]{1,0:T(8,128)(2,1)S(1)}, u32[]{:S(2)}, u32[]{:S(2)}) collective-permute-start(bf16[128,2048]{1,0:T(8,128)(2,1)S(1)} %collective-permute-done.4), channel_id=1, source_target_pairs={{1,0},{2,1},{3,2},{5,4},{6,5},{7,6},{9,8},{10,9},{11,10},{13,12},{... | collective-permute-start | bytes 1572872 | tf_op jit(solution)/shard_map/ppermute | solution.py:25
  62.0 10.8 %collective-permute-start.11 = (f32[256,896]{1,0:T(8,128)S(1)}, f32[256,896]{1,0:T(8,128)S(1)}, u32[]{:S(2)}, u32[]{:S(2)}) collective-permute-start(f32[256,896]{1,0:T(8,128)S(1)} %fusion.8), channel_id=1, source_target_pairs={{0,4},{4,0},{8,12},{12,8},{1,5},{5,1},{9,13},{13,9},{2,6},{6,2},{1... | collective-permute-start | bytes 2752520 | tf_op jit(solution)/shard_map/ppermute | solution.py:74
  62.1 12.6 %collective-permute-start.10 = (f32[256,896]{1,0:T(8,128)S(1)}, f32[256,896]{1,0:T(8,128)S(1)}, u32[]{:S(2)}, u32[]{:S(2)}) collective-permute-start(f32[256,896]{1,0:T(8,128)S(1)} %fusion.12), channel_id=1, source_target_pairs={{0,4},{4,0},{8,12},{12,8},{1,5},{5,1},{9,13},{13,9},{2,6},{6,2},{1... | collective-permute-start | bytes 2752520 | tf_op jit(solution)/shard_map/ppermute | solution.py:74
  66.3 11.4 %collective-permute-start.19 = (f32[256,896]{1,0:T(8,128)S(1)}, f32[256,896]{1,0:T(8,128)S(1)}, u32[]{:S(2)}, u32[]{:S(2)}) collective-permute-start(f32[256,896]{1,0:T(8,128)S(1)} %fusion), channel_id=1, source_target_pairs={{0,4},{4,0},{8,12},{12,8},{1,5},{5,1},{9,13},{13,9},{2,6},{6,2},{1... | collective-permute-start | bytes 2752520 | tf_op jit(solution)/shard_map/ppermute | solution.py:74
  68.6 10.9 %collective-permute-start.18 = (f32[256,896]{1,0:T(8,128)S(1)}, f32[256,896]{1,0:T(8,128)S(1)}, u32[]{:S(2)}, u32[]{:S(2)}) collective-permute-start(f32[256,896]{1,0:T(8,128)S(1)} %fusion.4), channel_id=1, source_target_pairs={{0,4},{4,0},{8,12},{12,8},{1,5},{5,1},{9,13},{13,9},{2,6},{6,2},{1... | collective-permute-start | bytes 2752520 | tf_op jit(solution)/shard_map/ppermute | solution.py:74
  69.8 12.8 %collective-permute-start.8 = (f32[2,64,768]{2,1,0:T(8,128)S(1)}, f32[2,64,768]{2,1,0:T(8,128)S(1)}, u32[]{:S(2)}, u32[]{:S(2)}) collective-permute-start(f32[2,64,768]{2,1,0:T(8,128)S(1)} %dynamic-slice_bitcast_fusion.3), channel_id=1, source_target_pairs={{0,8},{4,12},{8,0},{12,4},{1,9},{5,13},{9,1},{13,5},{2,10},{6,14},... | collective-permute-start | bytes 1179656 | tf_op jit(solution)/shard_map/ppermute | solution.py:62
  72.8 17.4 %collective-permute-start.16 = (f32[2,64,768]{2,1,0:T(8,128)S(1)}, f32[2,64,768]{2,1,0:T(8,128)S(1)}, u32[]{:S(2)}, u32[]{:S(2)}) collective-permute-start(f32[2,64,768]{2,1,0:T(8,128)S(1)} %dynamic-slice_bitcast_fusion.2), channel_id=1, source_target_pairs={{0,8},{4,12},{8,0},{12,4},{1,9},{5,13},{9,1},{13,5},{2,10},{6,14},... | collective-permute-start | bytes 1179656 | tf_op jit(solution)/shard_map/ppermute | solution.py:62
  74.7 17.2 %collective-permute-start.22 = (f32[2,64,768]{2,1,0:T(8,128)S(1)}, f32[2,64,768]{2,1,0:T(8,128)S(1)}, u32[]{:S(2)}, u32[]{:S(2)}) collective-permute-start(f32[2,64,768]{2,1,0:T(8,128)S(1)} %fusion.74), channel_id=1, source_target_pairs={{0,16},{16,0},{1,17},{17,1},{2,18},{18,2},{3,19},{19,3},{4,20},{20... | collective-permute-start | bytes 1179656 | tf_op jit(solution)/shard_map/ppermute | solution.py:66
  77.7 17.4 %collective-permute-start.26 = (f32[2,64,768]{2,1,0:T(8,128)S(1)}, f32[2,64,768]{2,1,0:T(8,128)S(1)}, u32[]{:S(2)}, u32[]{:S(2)}) collective-permute-start(f32[2,64,768]{2,1,0:T(8,128)S(1)} %fusion.79), channel_id=1, source_target_pairs={{0,16},{16,0},{1,17},{17,1},{2,18},{18,2},{3,19},{19,3},{4,20},{20... | collective-permute-start | bytes 1179656 | tf_op jit(solution)/shard_map/ppermute | solution.py:66
  81.1 19.1 %collective-permute-start.12 = (f32[2,64,896]{2,1,0:T(8,128)S(1)}, f32[2,64,896]{2,1,0:T(8,128)S(1)}, u32[]{:S(2)}, u32[]{:S(2)}) collective-permute-start(f32[2,64,896]{2,1,0:T(8,128)S(1)} %dynamic-slice_bitcast_fusion.1), channel_id=1, source_target_pairs={{0,8},{4,12},{8,0},{12,4},{1,9},{5,13},{9,1},{13,5},{2,10},{6,14},... | collective-permute-start | bytes 1376264 | tf_op jit(solution)/shard_map/ppermute | solution.py:62
  82.7 26.7 %collective-permute-start.20 = (f32[2,64,896]{2,1,0:T(8,128)S(1)}, f32[2,64,896]{2,1,0:T(8,128)S(1)}, u32[]{:S(2)}, u32[]{:S(2)}) collective-permute-start(f32[2,64,896]{2,1,0:T(8,128)S(1)} %dynamic-slice_bitcast_fusion), channel_id=1, source_target_pairs={{0,8},{4,12},{8,0},{12,4},{1,9},{5,13},{9,1},{13,5},{2,10},{6,14},... | collective-permute-start | bytes 1376264 | tf_op jit(solution)/shard_map/ppermute | solution.py:62
  90.3 20.7 %collective-permute-start.24 = (f32[2,64,896]{2,1,0:T(8,128)S(1)}, f32[2,64,896]{2,1,0:T(8,128)S(1)}, u32[]{:S(2)}, u32[]{:S(2)}) collective-permute-start(f32[2,64,896]{2,1,0:T(8,128)S(1)} %fusion.64), channel_id=1, source_target_pairs={{0,16},{16,0},{1,17},{17,1},{2,18},{18,2},{3,19},{19,3},{4,20},{20... | collective-permute-start | bytes 1376264 | tf_op jit(solution)/shard_map/ppermute | solution.py:66
  91.9 22.9 %collective-permute-start.28 = (f32[2,64,896]{2,1,0:T(8,128)S(1)}, f32[2,64,896]{2,1,0:T(8,128)S(1)}, u32[]{:S(2)}, u32[]{:S(2)}) collective-permute-start(f32[2,64,896]{2,1,0:T(8,128)S(1)} %fusion.69), channel_id=1, source_target_pairs={{0,16},{16,0},{1,17},{17,1},{2,18},{18,2},{3,19},{19,3},{4,20},{20... | collective-permute-start | bytes 1376264 | tf_op jit(solution)/shard_map/ppermute | solution.py:66
  95.2 23.9 %collective-permute-start.9 = (f32[64,768]{1,0:T(8,128)S(1)}, f32[64,768]{1,0:T(8,128)S(1)}, u32[]{:S(2)}, u32[]{:S(2)}) collective-permute-start(f32[64,768]{1,0:T(8,128)S(1)} %dynamic-slice_bitcast_fusion.11), channel_id=1, source_target_pairs={{0,16},{16,0},{1,17},{17,1},{2,18},{18,2},{3,19},{19,3},{4,20},{20... | collective-permute-start | bytes 589832 | tf_op jit(solution)/shard_map/ppermute | solution.py:66
  100.1 23.2 %collective-permute-start.17 = (f32[64,768]{1,0:T(8,128)S(1)}, f32[64,768]{1,0:T(8,128)S(1)}, u32[]{:S(2)}, u32[]{:S(2)}) collective-permute-start(f32[64,768]{1,0:T(8,128)S(1)} %dynamic-slice_bitcast_fusion.10), channel_id=1, source_target_pairs={{0,16},{16,0},{1,17},{17,1},{2,18},{18,2},{3,19},{19,3},{4,20},{20... | collective-permute-start | bytes 589832 | tf_op jit(solution)/shard_map/ppermute | solution.py:66
  109.3 15.4 %collective-permute-start.23 = (f32[64,768]{1,0:T(8,128)S(1)}, f32[64,768]{1,0:T(8,128)S(1)}, u32[]{:S(2)}, u32[]{:S(2)}) collective-permute-start(f32[64,768]{1,0:T(8,128)S(1)} %dynamic-slice_bitcast_fusion.9), channel_id=1, source_target_pairs={{0,8},{4,12},{8,0},{12,4},{1,9},{5,13},{9,1},{13,5},{2,10},{6,14},... | collective-permute-start | bytes 589832 | tf_op jit(solution)/shard_map/ppermute | solution.py:62
  111.0 14.4 %collective-permute-start.27 = (f32[64,768]{1,0:T(8,128)S(1)}, f32[64,768]{1,0:T(8,128)S(1)}, u32[]{:S(2)}, u32[]{:S(2)}) collective-permute-start(f32[64,768]{1,0:T(8,128)S(1)} %dynamic-slice_bitcast_fusion.8), channel_id=1, source_target_pairs={{0,8},{4,12},{8,0},{12,4},{1,9},{5,13},{9,1},{13,5},{2,10},{6,14},... | collective-permute-start | bytes 589832 | tf_op jit(solution)/shard_map/ppermute | solution.py:62
  114.8 13.3 %collective-permute-start.13 = (f32[64,896]{1,0:T(8,128)S(1)}, f32[64,896]{1,0:T(8,128)S(1)}, u32[]{:S(2)}, u32[]{:S(2)}) collective-permute-start(f32[64,896]{1,0:T(8,128)S(1)} %dynamic-slice_bitcast_fusion.7), channel_id=1, source_target_pairs={{0,16},{16,0},{1,17},{17,1},{2,18},{18,2},{3,19},{19,3},{4,20},{20... | collective-permute-start | bytes 688136 | tf_op jit(solution)/shard_map/ppermute | solution.py:66
  119.1 12.9 %collective-permute-start.21 = (f32[64,896]{1,0:T(8,128)S(1)}, f32[64,896]{1,0:T(8,128)S(1)}, u32[]{:S(2)}, u32[]{:S(2)}) collective-permute-start(f32[64,896]{1,0:T(8,128)S(1)} %dynamic-slice_bitcast_fusion.6), channel_id=1, source_target_pairs={{0,16},{16,0},{1,17},{17,1},{2,18},{18,2},{3,19},{19,3},{4,20},{20... | collective-permute-start | bytes 688136 | tf_op jit(solution)/shard_map/ppermute | solution.py:66
  (8 other events, 93.5 us)

commit v4 on v3

--- a/solution.py
+++ b/solution.py
@@ -15,7 +15,7 @@
     return buf
 
 
-def gather_tokens(tokens, n_col, col):
+def relay_tokens(tokens, n_col):
     rightward = [(q, q + 1) for q in range(n_col - 1)]
     leftward = [(q + 1, q) for q in range(n_col - 1)]
     from_left, from_right = [], []
@@ -25,6 +25,11 @@
         going_left = lax.ppermute(going_left, "col", leftward)
         from_left.append(going_right)
         from_right.append(going_left)
+    return from_left, from_right
+
+
+def gather_tokens(tokens, n_col, col):
+    from_left, from_right = relay_tokens(tokens, n_col)
     line = jnp.stack(from_left[::-1] + [tokens] + from_right)
     gathered = lax.dynamic_slice_in_dim(line, n_col - 1 - col, n_col, 0)
     return gathered.reshape(n_col * tokens.shape[0], tokens.shape[1])
@@ -41,8 +46,7 @@
     hi = row // 2
     n_hi = n_row // 2
 
-    gathered = gather_tokens(tokens, n_col, col)
-    total = gathered.shape[0]
+    total = tokens.shape[0] * n_col
     width = weight.shape[1]
     block = total // n_row
     part = width // n_depth
@@ -50,10 +54,6 @@
     lanes = part // 128 if part % 128 == 0 else 1
     chunks = min(4, lanes)
     bounds = [(lanes * q // chunks) * (part // lanes) for q in range(chunks + 1)]
-
-    by_block = gathered.reshape(n_hi, 2, block, gathered.shape[1])
-    own_rows = lax.dynamic_index_in_dim(by_block, core, 1, keepdims=False).reshape(n_hi * block, -1)
-    other_rows = lax.dynamic_index_in_dim(by_block, 1 - core, 1, keepdims=False).reshape(n_hi * block, -1)
 
     partner = [(q, q ^ 1) for q in range(n_row)]
 
@@ -67,6 +67,39 @@
 
     def columns(d, q):
         return weight[:, d * part + bounds[q]:d * part + bounds[q + 1]]
+
+    if n_row == 4 and n_col == 4 and block == tokens.shape[0]:
+        from_left, from_right = relay_tokens(tokens, n_col)
+        even = col % 2 == 0
+        low = col < 2
+        mine = col % 2 == core
+        next_block = jnp.where(even, from_right[0], from_left[0])
+        far_block = jnp.where(low, from_right[1], from_left[1])
+        last_block = jnp.where(
+            col == 0, from_right[2],
+            jnp.where(col == 1, from_right[0], jnp.where(col == 2, from_left[0], from_left[2])),
+        )
+
+        def stage(kept_tokens, sent_tokens):
+            both = jnp.concatenate([sent_tokens, kept_tokens])
+            pieces = []
+            for q in range(chunks):
+                products = [jnp.dot(both, columns(d, q), preferred_element_type=jnp.float32) for d in range(n_depth)]
+                arrived = lax.ppermute([p[:block] for p in products], "row", partner)
+                summed = jnp.stack([p[block:] + a for p, a in zip(products, arrived)])
+                pair = ring_reduce_scatter(summed, 0, n_depth, depth, shift_depth)
+                pieces.append(pair + shift_hi(pair))
+            return jnp.concatenate(pieces, axis=1)
+
+        first = stage(jnp.where(mine, tokens, next_block), jnp.where(mine, next_block, tokens))
+        second = stage(jnp.where(mine, far_block, last_block), jnp.where(mine, last_block, far_block))
+        shares = jnp.where(hi == col // 2, first, second)
+        return shares.astype(jnp.bfloat16).reshape(block, 1, part)
+
+    gathered = gather_tokens(tokens, n_col, col)
+    by_block = gathered.reshape(n_hi, 2, block, gathered.shape[1])
+    own_rows = lax.dynamic_index_in_dim(by_block, core, 1, keepdims=False).reshape(n_hi * block, -1)
+    other_rows = lax.dynamic_index_in_dim(by_block, 1 - core, 1, keepdims=False).reshape(n_hi * block, -1)
 
     firsts, seconds = [], []
     for q in range(chunks):

time: 135 us -> 207 us (1.53)
  waiting for transfers between devices: 68.9 us -> 130 us
  matrix products: 22.8 us -> 29.5 us
  other arithmetic: 2.43 us -> 5.31 us
    ppermute x8, waiting for transfers between devices: 17.4 us -> 61.3 us  [shift_depth(): return lax.ppermute(value, 'depth', pairs)]
    ppermute x8, waiting for transfers between devices: 19.2 us -> 36.4 us  [shift_hi(): return lax.ppermute(value, 'row', pairs)]
    dot_general x16, matrix products: 22.8 us -> 29.5 us  [stage(): jnp.dot(both, columns(d, q), preferred_element_type=jnp.float32)]
    ppermute x14 -> x22, starting transfers between devices: 19.6 us -> 22.5 us  [the longest x3 14.8 us: relay_tokens(): going_right = lax.ppermute(going_right, 'col', rightward)]
    ppermute x14 -> x22, waiting for transfers between devices: 32.3 us -> 32.7 us  [the longest x3 27.4 us: relay_tokens(): going_left = lax.ppermute(going_left, 'col', leftward)]
  transfers between devices with their start and end apart: 30 -> 38, of which waited for: 15 -> 22; matrix products, arithmetic and copies ran while one was open for 10% -> 4% of each run, Pallas kernels for 0% -> 0%
where the time goes in v4:
time: 207 us; the launch traced here: 206 us
  waiting for transfers between devices  130 us (63%)
  starting transfers between devices  40 us (19%)
  matrix products  29.5 us (14%)
  other arithmetic  5.31 us (3%)
    ppermute x8, waiting for transfers between devices, shift_depth(): return lax.ppermute(value, 'depth', pairs)  61.3 us
    ppermute x8, waiting for transfers between devices, shift_hi(): return lax.ppermute(value, 'row', pairs)  36.4 us
    dot_general x16, matrix products, stage(): jnp.dot(both, columns(d, q), preferred_element_type=jnp.float32)  29.5 us
    ppermute x3, waiting for transfers between devices, relay_tokens(): going_left = lax.ppermute(going_left, 'col', leftward)  27.4 us
    ppermute x3, starting transfers between devices, relay_tokens(): going_right = lax.ppermute(going_right, 'col', rightward)  14.8 us
    ppermute x8, starting transfers between devices, shift_depth(): return lax.ppermute(value, 'depth', pairs)  8.85 us
    ppermute x8, starting transfers between devices, shift_hi(): return lax.ppermute(value, 'row', pairs)  8.65 us
  transfers between devices with their start and end apart: 38, of which 22 were waited for; matrix products, arithmetic and copies ran while one was open for 4% of the time, Pallas kernels for 0%

profile of v4, /device:TPU:0, one launch (start us, length us, event | category | flops | bytes accessed | tf_op | source)
XLA Modules:
  0.0 206.4 jit_solution(3679455483095036297)
XLA Ops:
  1.3 5.6 %collective-permute-start.1 = (bf16[128,2048]{1,0:T(8,128)(2,1)}, bf16[128,2048]{1,0:T(8,128)(2,1)S(1)}, u32[]{:S(2)}, u32[]{:S(2)}) collective-permute-start(bf16[128,2048]{1,0:T(8,128)(2,1)} %param.2), channel_id=1, source_target_pairs={{0,1},{1,2},{2,3},{4,5},{5,6},{6,7},{8,9},{9,10},{10,11},{12,13},{... | collective-permute-start | bytes 1572872 | tf_op jit(solution)/shard_map/ppermute | solution.py:24
  6.9 10.2 %collective-permute-done = bf16[128,2048]{1,0:T(8,128)(2,1)S(1)} collective-permute-done((bf16[128,2048]{1,0:T(8,128)(2,1)}, bf16[128,2048]{1,0:T(8,128)(2,1)S(1)}, u32[]{:S(2)}, u32[]{:S(2)}) %collective-permute-start) | collective-permute-done | bytes 524320 | tf_op jit(solution)/shard_map/ppermute | solution.py:25
  18.4 4.6 %collective-permute-start.20 = (bf16[128,2048]{1,0:T(8,128)(2,1)S(1)}, bf16[128,2048]{1,0:T(8,128)(2,1)S(1)}, u32[]{:S(2)}, u32[]{:S(2)}) collective-permute-start(bf16[128,2048]{1,0:T(8,128)(2,1)S(1)} %collective-permute-done.1), channel_id=1, source_target_pairs={{0,1},{1,2},{2,3},{4,5},{5,6},{6,7},{8,9},{9,10},{10,11},{12,13},{... | collective-permute-start | bytes 1572872 | tf_op jit(solution)/shard_map/ppermute | solution.py:24
  23.0 9.1 %collective-permute-done.18 = bf16[128,2048]{1,0:T(8,128)(2,1)S(1)} collective-permute-done((bf16[128,2048]{1,0:T(8,128)(2,1)S(1)}, bf16[128,2048]{1,0:T(8,128)(2,1)S(1)}, u32[]{:S(2)}, u32[]{:S(2)}) %collective-permute-start.18) | collective-permute-done | bytes 524320 | tf_op jit(solution)/shard_map/ppermute | solution.py:25
  33.3 4.6 %collective-permute-start.21 = (bf16[128,2048]{1,0:T(8,128)(2,1)S(1)}, bf16[128,2048]{1,0:T(8,128)(2,1)S(1)}, u32[]{:S(2)}, u32[]{:S(2)}) collective-permute-start(bf16[128,2048]{1,0:T(8,128)(2,1)S(1)} %collective-permute-done.20), channel_id=1, source_target_pairs={{0,1},{1,2},{2,3},{4,5},{5,6},{6,7},{8,9},{9,10},{10,11},{12,13},{... | collective-permute-start | bytes 1572872 | tf_op jit(solution)/shard_map/ppermute | solution.py:24
  38.0 8.1 %collective-permute-done.19 = bf16[128,2048]{1,0:T(8,128)(2,1)S(1)} collective-permute-done((bf16[128,2048]{1,0:T(8,128)(2,1)S(1)}, bf16[128,2048]{1,0:T(8,128)(2,1)S(1)}, u32[]{:S(2)}, u32[]{:S(2)}) %collective-permute-start.19) | collective-permute-done | bytes 524320 | tf_op jit(solution)/shard_map/ppermute | solution.py:25
  48.9 3.2 %fusion.24 = f32[256,768]{1,0:T(8,128)S(1)} fusion(bf16[2048,6656]{1,0:T(8,128)(2,1)} %param.3, bf16[128,2048]{1,0:T(8,128)(2,1)S(1)} %broadcast_select_fusion.2, bf16[128,2048]{1,0:T(8,128)(2,1)S(1)} %get-tuple-element.5), kind=kOutput, calls=%fused_computation.24 | convolution fusion | flops 807403520 | bytes 4980736 | tf_op jit(solution)/shard_map/dot_general | solution.py:87
  52.1 3.6 %fusion.28 = f32[256,768]{1,0:T(8,128)S(1)} fusion(bf16[2048,6656]{1,0:T(8,128)(2,1)} %param.3, bf16[128,2048]{1,0:T(8,128)(2,1)S(1)} %broadcast_select_fusion.2, bf16[128,2048]{1,0:T(8,128)(2,1)S(1)} %get-tuple-element.5), kind=kOutput, calls=%fused_computation.28 | convolution fusion | flops 807403520 | bytes 4980736 | tf_op jit(solution)/shard_map/dot_general | solution.py:87
  55.8 4.1 %fusion.8 = f32[256,896]{1,0:T(8,128)S(1)} fusion(bf16[2048,6656]{1,0:T(8,128)(2,1)} %param.3, bf16[128,2048]{1,0:T(8,128)(2,1)S(1)} %broadcast_select_fusion.2, bf16[128,2048]{1,0:T(8,128)(2,1)S(1)} %get-tuple-element.5), kind=kOutput, calls=%fused_computation.8 | convolution fusion | flops 941621248 | bytes 5636096 | tf_op jit(solution)/shard_map/dot_general | solution.py:87
  70.0 1.5 fusion.2
  72.9 2.9 %fusion.18 = f32[256,768]{1,0:T(8,128)S(1)} fusion(bf16[2048,6656]{1,0:T(8,128)(2,1)} %param.3, bf16[128,2048]{1,0:T(8,128)(2,1)S(1)} %get-tuple-element.9, bf16[128,2048]{1,0:T(8,128)(2,1)S(1)} %get-tuple-element.10), kind=kOutput, calls=%fused_computation.18 | convolution fusion | flops 807403520 | bytes 4980736 | tf_op jit(solution)/shard_map/dot_general | solution.py:87
  76.4 2.9 %fusion.22 = f32[256,768]{1,0:T(8,128)S(1)} fusion(bf16[2048,6656]{1,0:T(8,128)(2,1)} %param.3, bf16[128,2048]{1,0:T(8,128)(2,1)S(1)} %get-tuple-element.9, bf16[128,2048]{1,0:T(8,128)(2,1)S(1)} %get-tuple-element.10), kind=kOutput, calls=%fused_computation.22 | convolution fusion | flops 807403520 | bytes 4980736 | tf_op jit(solution)/shard_map/dot_general | solution.py:87
  94.4 5.9 %collective-permute-done.24 = f32[128,768]{1,0:T(8,128)S(1)} collective-permute-done((f32[128,768]{1,0:T(8,128)S(1)}, f32[128,768]{1,0:T(8,128)S(1)}, u32[]{:S(2)}, u32[]{:S(2)}) %collective-permute-start.24) | collective-permute-done | bytes 393248 | tf_op jit(solution)/shard_map/ppermute | solution.py:66
  101.5 7.2 %collective-permute-done.32 = f32[128,768]{1,0:T(8,128)S(1)} collective-permute-done((f32[128,768]{1,0:T(8,128)S(1)}, f32[128,768]{1,0:T(8,128)S(1)}, u32[]{:S(2)}, u32[]{:S(2)}) %collective-permute-start.32) | collective-permute-done | bytes 393248 | tf_op jit(solution)/shard_map/ppermute | solution.py:66
  109.9 7.2 %collective-permute-done.4 = f32[128,768]{1,0:T(8,128)S(1)} collective-permute-done((f32[128,768]{1,0:T(8,128)S(1)}, f32[128,768]{1,0:T(8,128)S(1)}, u32[]{:S(2)}, u32[]{:S(2)}) %collective-permute-start.4) | collective-permute-done | bytes 393248 | tf_op jit(solution)/shard_map/ppermute | solution.py:66
  118.4 7.2 %collective-permute-done.12 = f32[128,768]{1,0:T(8,128)S(1)} collective-permute-done((f32[128,768]{1,0:T(8,128)S(1)}, f32[128,768]{1,0:T(8,128)S(1)}, u32[]{:S(2)}, u32[]{:S(2)}) %collective-permute-start.12) | collective-permute-done | bytes 393248 | tf_op jit(solution)/shard_map/ppermute | solution.py:66
  126.8 8.6 %collective-permute-done.28 = f32[128,896]{1,0:T(8,128)S(1)} collective-permute-done((f32[128,896]{1,0:T(8,128)S(1)}, f32[128,896]{1,0:T(8,128)S(1)}, u32[]{:S(2)}, u32[]{:S(2)}) %collective-permute-start.28) | collective-permute-done | bytes 458784 | tf_op jit(solution)/shard_map/ppermute | solution.py:66
  136.6 8.6 %collective-permute-done.36 = f32[128,896]{1,0:T(8,128)S(1)} collective-permute-done((f32[128,896]{1,0:T(8,128)S(1)}, f32[128,896]{1,0:T(8,128)S(1)}, u32[]{:S(2)}, u32[]{:S(2)}) %collective-permute-start.36) | collective-permute-done | bytes 458784 | tf_op jit(solution)/shard_map/ppermute | solution.py:66
  146.5 8.6 %collective-permute-done.8 = f32[128,896]{1,0:T(8,128)S(1)} collective-permute-done((f32[128,896]{1,0:T(8,128)S(1)}, f32[128,896]{1,0:T(8,128)S(1)}, u32[]{:S(2)}, u32[]{:S(2)}) %collective-permute-start.8) | collective-permute-done | bytes 458784 | tf_op jit(solution)/shard_map/ppermute | solution.py:66
  156.3 7.8 %collective-permute-done.16 = f32[128,896]{1,0:T(8,128)S(1)} collective-permute-done((f32[128,896]{1,0:T(8,128)S(1)}, f32[128,896]{1,0:T(8,128)S(1)}, u32[]{:S(2)}, u32[]{:S(2)}) %collective-permute-start.16) | collective-permute-done | bytes 458784 | tf_op jit(solution)/shard_map/ppermute | solution.py:66
  168.7 8.8 %collective-permute-done.29 = f32[128,896]{1,0:T(8,128)S(1)} collective-permute-done((f32[128,896]{1,0:T(8,128)S(1)}, f32[128,896]{1,0:T(8,128)S(1)}, u32[]{:S(2)}, u32[]{:S(2)}) %collective-permute-start.29) | collective-permute-done | bytes 458784 | tf_op jit(solution)/shard_map/ppermute | solution.py:62
  177.5 9.8 %collective-permute-done.37 = f32[128,896]{1,0:T(8,128)S(1)} collective-permute-done((f32[128,896]{1,0:T(8,128)S(1)}, f32[128,896]{1,0:T(8,128)S(1)}, u32[]{:S(2)}, u32[]{:S(2)}) %collective-permute-start.37) | collective-permute-done | bytes 458784 | tf_op jit(solution)/shard_map/ppermute | solution.py:62
  187.4 9.8 %collective-permute-done.9 = f32[128,896]{1,0:T(8,128)S(1)} collective-permute-done((f32[128,896]{1,0:T(8,128)S(1)}, f32[128,896]{1,0:T(8,128)S(1)}, u32[]{:S(2)}, u32[]{:S(2)}) %collective-permute-start.9) | collective-permute-done | bytes 458784 | tf_op jit(solution)/shard_map/ppermute | solution.py:62
  197.2 8.1 %collective-permute-done.17 = f32[128,896]{1,0:T(8,128)S(1)} collective-permute-done((f32[128,896]{1,0:T(8,128)S(1)}, f32[128,896]{1,0:T(8,128)S(1)}, u32[]{:S(2)}, u32[]{:S(2)}) %collective-permute-start.17) | collective-permute-done | bytes 458784 | tf_op jit(solution)/shard_map/ppermute | solution.py:62
  (129 shorter events, 47.8 us)
Async XLA Ops:
  0.0 17.1 %collective-permute-start = (bf16[128,2048]{1,0:T(8,128)(2,1)}, bf16[128,2048]{1,0:T(8,128)(2,1)S(1)}, u32[]{:S(2)}, u32[]{:S(2)}) collective-permute-start(bf16[128,2048]{1,0:T(8,128)(2,1)} %param.2), channel_id=1, source_target_pairs={{1,0},{2,1},{3,2},{5,4},{6,5},{7,6},{9,8},{10,9},{11,10},{13,12},{... | collective-permute-start | bytes 1572872 | tf_op jit(solution)/shard_map/ppermute | solution.py:25
  1.3 17.1 %collective-permute-start.1 = (bf16[128,2048]{1,0:T(8,128)(2,1)}, bf16[128,2048]{1,0:T(8,128)(2,1)S(1)}, u32[]{:S(2)}, u32[]{:S(2)}) collective-permute-start(bf16[128,2048]{1,0:T(8,128)(2,1)} %param.2), channel_id=1, source_target_pairs={{0,1},{1,2},{2,3},{4,5},{5,6},{6,7},{8,9},{9,10},{10,11},{12,13},{... | collective-permute-start | bytes 1572872 | tf_op jit(solution)/shard_map/ppermute | solution.py:24
  17.1 15.0 %collective-permute-start.18 = (bf16[128,2048]{1,0:T(8,128)(2,1)S(1)}, bf16[128,2048]{1,0:T(8,128)(2,1)S(1)}, u32[]{:S(2)}, u32[]{:S(2)}) collective-permute-start(bf16[128,2048]{1,0:T(8,128)(2,1)S(1)} %collective-permute-done), channel_id=1, source_target_pairs={{1,0},{2,1},{3,2},{5,4},{6,5},{7,6},{9,8},{10,9},{11,10},{13,12},{... | collective-permute-start | bytes 1572872 | tf_op jit(solution)/shard_map/ppermute | solution.py:25
  18.4 15.0 %collective-permute-start.20 = (bf16[128,2048]{1,0:T(8,128)(2,1)S(1)}, bf16[128,2048]{1,0:T(8,128)(2,1)S(1)}, u32[]{:S(2)}, u32[]{:S(2)}) collective-permute-start(bf16[128,2048]{1,0:T(8,128)(2,1)S(1)} %collective-permute-done.1), channel_id=1, source_target_pairs={{0,1},{1,2},{2,3},{4,5},{5,6},{6,7},{8,9},{9,10},{10,11},{12,13},{... | collective-permute-start | bytes 1572872 | tf_op jit(solution)/shard_map/ppermute | solution.py:24
  32.0 14.1 %collective-permute-start.19 = (bf16[128,2048]{1,0:T(8,128)(2,1)S(1)}, bf16[128,2048]{1,0:T(8,128)(2,1)S(1)}, u32[]{:S(2)}, u32[]{:S(2)}) collective-permute-start(bf16[128,2048]{1,0:T(8,128)(2,1)S(1)} %collective-permute-done.18), channel_id=1, source_target_pairs={{1,0},{2,1},{3,2},{5,4},{6,5},{7,6},{9,8},{10,9},{11,10},{13,12},{... | collective-permute-start | bytes 1572872 | tf_op jit(solution)/shard_map/ppermute | solution.py:25
  33.3 14.0 %collective-permute-start.21 = (bf16[128,2048]{1,0:T(8,128)(2,1)S(1)}, bf16[128,2048]{1,0:T(8,128)(2,1)S(1)}, u32[]{:S(2)}, u32[]{:S(2)}) collective-permute-start(bf16[128,2048]{1,0:T(8,128)(2,1)S(1)} %collective-permute-done.20), channel_id=1, source_target_pairs={{0,1},{1,2},{2,3},{4,5},{5,6},{6,7},{8,9},{9,10},{10,11},{12,13},{... | collective-permute-start | bytes 1572872 | tf_op jit(solution)/shard_map/ppermute | solution.py:24
  72.8 7.7 %collective-permute-start.23 = (f32[128,768]{1,0:T(8,128)S(1)}, f32[128,768]{1,0:T(8,128)S(1)}, u32[]{:S(2)}, u32[]{:S(2)}) collective-permute-start(f32[128,768]{1,0:T(8,128)S(1)} %slice.187), channel_id=1, source_target_pairs={{0,4},{4,0},{8,12},{12,8},{1,5},{5,1},{9,13},{13,9},{2,6},{6,2},{1... | collective-permute-start | bytes 1179656 | tf_op jit(solution)/shard_map/ppermute | solution.py:88
  79.4 7.9 %collective-permute-start.26 = (f32[128,896]{1,0:T(8,128)S(1)}, f32[128,896]{1,0:T(8,128)S(1)}, u32[]{:S(2)}, u32[]{:S(2)}) collective-permute-start(f32[128,896]{1,0:T(8,128)S(1)} %slice.189), channel_id=1, source_target_pairs={{0,4},{4,0},{8,12},{12,8},{1,5},{5,1},{9,13},{13,9},{2,6},{6,2},{1... | collective-permute-start | bytes 1376264 | tf_op jit(solution)/shard_map/ppermute | solution.py:88
  88.3 12.1 %collective-permute-start.24 = (f32[128,768]{1,0:T(8,128)S(1)}, f32[128,768]{1,0:T(8,128)S(1)}, u32[]{:S(2)}, u32[]{:S(2)}) collective-permute-start(f32[128,768]{1,0:T(8,128)S(1)} %fusion.70), channel_id=1, source_target_pairs={{0,16},{16,0},{1,17},{17,1},{2,18},{18,2},{3,19},{19,3},{4,20},{20... | collective-permute-start | bytes 1179656 | tf_op jit(solution)/shard_map/ppermute | solution.py:66
  89.5 19.2 %collective-permute-start.32 = (f32[128,768]{1,0:T(8,128)S(1)}, f32[128,768]{1,0:T(8,128)S(1)}, u32[]{:S(2)}, u32[]{:S(2)}) collective-permute-start(f32[128,768]{1,0:T(8,128)S(1)} %fusion.65), channel_id=1, source_target_pairs={{0,16},{16,0},{1,17},{17,1},{2,18},{18,2},{3,19},{19,3},{4,20},{20... | collective-permute-start | bytes 1179656 | tf_op jit(solution)/shard_map/ppermute | solution.py:66
  90.5 26.6 %collective-permute-start.4 = (f32[128,768]{1,0:T(8,128)S(1)}, f32[128,768]{1,0:T(8,128)S(1)}, u32[]{:S(2)}, u32[]{:S(2)}) collective-permute-start(f32[128,768]{1,0:T(8,128)S(1)} %fusion.80), channel_id=1, source_target_pairs={{0,16},{16,0},{1,17},{17,1},{2,18},{18,2},{3,19},{19,3},{4,20},{20... | collective-permute-start | bytes 1179656 | tf_op jit(solution)/shard_map/ppermute | solution.py:66
  91.8 33.8 %collective-permute-start.12 = (f32[128,768]{1,0:T(8,128)S(1)}, f32[128,768]{1,0:T(8,128)S(1)}, u32[]{:S(2)}, u32[]{:S(2)}) collective-permute-start(f32[128,768]{1,0:T(8,128)S(1)} %fusion.75), channel_id=1, source_target_pairs={{0,16},{16,0},{1,17},{17,1},{2,18},{18,2},{3,19},{19,3},{4,20},{20... | collective-permute-start | bytes 1179656 | tf_op jit(solution)/shard_map/ppermute | solution.py:66
  92.8 42.6 %collective-permute-start.28 = (f32[128,896]{1,0:T(8,128)S(1)}, f32[128,896]{1,0:T(8,128)S(1)}, u32[]{:S(2)}, u32[]{:S(2)}) collective-permute-start(f32[128,896]{1,0:T(8,128)S(1)} %fusion.42), channel_id=1, source_target_pairs={{0,16},{16,0},{1,17},{17,1},{2,18},{18,2},{3,19},{19,3},{4,20},{20... | collective-permute-start | bytes 1376264 | tf_op jit(solution)/shard_map/ppermute | solution.py:66
  100.3 44.9 %collective-permute-start.36 = (f32[128,896]{1,0:T(8,128)S(1)}, f32[128,896]{1,0:T(8,128)S(1)}, u32[]{:S(2)}, u32[]{:S(2)}) collective-permute-start(f32[128,896]{1,0:T(8,128)S(1)} %fusion.37), channel_id=1, source_target_pairs={{0,16},{16,0},{1,17},{17,1},{2,18},{18,2},{3,19},{19,3},{4,20},{20... | collective-permute-start | bytes 1376264 | tf_op jit(solution)/shard_map/ppermute | solution.py:66
  108.7 46.3 %collective-permute-start.8 = (f32[128,896]{1,0:T(8,128)S(1)}, f32[128,896]{1,0:T(8,128)S(1)}, u32[]{:S(2)}, u32[]{:S(2)}) collective-permute-start(f32[128,896]{1,0:T(8,128)S(1)} %fusion.52), channel_id=1, source_target_pairs={{0,16},{16,0},{1,17},{17,1},{2,18},{18,2},{3,19},{19,3},{4,20},{20... | collective-permute-start | bytes 1376264 | tf_op jit(solution)/shard_map/ppermute | solution.py:66
  117.2 46.9 %collective-permute-start.16 = (f32[128,896]{1,0:T(8,128)S(1)}, f32[128,896]{1,0:T(8,128)S(1)}, u32[]{:S(2)}, u32[]{:S(2)}) collective-permute-start(f32[128,896]{1,0:T(8,128)S(1)} %fusion.47), channel_id=1, source_target_pairs={{0,16},{16,0},{1,17},{17,1},{2,18},{18,2},{3,19},{19,3},{4,20},{20... | collective-permute-start | bytes 1376264 | tf_op jit(solution)/shard_map/ppermute | solution.py:66
  125.6 39.7 %collective-permute-start.25 = (f32[128,768]{1,0:T(8,128)S(1)}, f32[128,768]{1,0:T(8,128)S(1)}, u32[]{:S(2)}, u32[]{:S(2)}) collective-permute-start(f32[128,768]{1,0:T(8,128)S(1)} %fusion.68), channel_id=1, source_target_pairs={{0,8},{4,12},{8,0},{12,4},{1,9},{5,13},{9,1},{13,5},{2,10},{6,14},... | collective-permute-start | bytes 1179656 | tf_op jit(solution)/shard_map/ppermute | solution.py:62
  135.4 30.9 %collective-permute-start.33 = (f32[128,768]{1,0:T(8,128)S(1)}, f32[128,768]{1,0:T(8,128)S(1)}, u32[]{:S(2)}, u32[]{:S(2)}) collective-permute-start(f32[128,768]{1,0:T(8,128)S(1)} %fusion.63), channel_id=1, source_target_pairs={{0,8},{4,12},{8,0},{12,4},{1,9},{5,13},{9,1},{13,5},{2,10},{6,14},... | collective-permute-start | bytes 1179656 | tf_op jit(solution)/shard_map/ppermute | solution.py:62
  145.2 22.3 %collective-permute-start.5 = (f32[128,768]{1,0:T(8,128)S(1)}, f32[128,768]{1,0:T(8,128)S(1)}, u32[]{:S(2)}, u32[]{:S(2)}) collective-permute-start(f32[128,768]{1,0:T(8,128)S(1)} %fusion.78), channel_id=1, source_target_pairs={{0,8},{4,12},{8,0},{12,4},{1,9},{5,13},{9,1},{13,5},{2,10},{6,14},... | collective-permute-start | bytes 1179656 | tf_op jit(solution)/shard_map/ppermute | solution.py:62
  155.1 13.5 %collective-permute-start.13 = (f32[128,768]{1,0:T(8,128)S(1)}, f32[128,768]{1,0:T(8,128)S(1)}, u32[]{:S(2)}, u32[]{:S(2)}) collective-permute-start(f32[128,768]{1,0:T(8,128)S(1)} %fusion.73), channel_id=1, source_target_pairs={{0,8},{4,12},{8,0},{12,4},{1,9},{5,13},{9,1},{13,5},{2,10},{6,14},... | collective-permute-start | bytes 1179656 | tf_op jit(solution)/shard_map/ppermute | solution.py:62
  164.1 13.4 %collective-permute-start.29 = (f32[128,896]{1,0:T(8,128)S(1)}, f32[128,896]{1,0:T(8,128)S(1)}, u32[]{:S(2)}, u32[]{:S(2)}) collective-permute-start(f32[128,896]{1,0:T(8,128)S(1)} %fusion.40), channel_id=1, source_target_pairs={{0,8},{4,12},{8,0},{12,4},{1,9},{5,13},{9,1},{13,5},{2,10},{6,14},... | collective-permute-start | bytes 1376264 | tf_op jit(solution)/shard_map/ppermute | solution.py:62
  165.3 22.0 %collective-permute-start.37 = (f32[128,896]{1,0:T(8,128)S(1)}, f32[128,896]{1,0:T(8,128)S(1)}, u32[]{:S(2)}, u32[]{:S(2)}) collective-permute-start(f32[128,896]{1,0:T(8,128)S(1)} %fusion.35), channel_id=1, source_target_pairs={{0,8},{4,12},{8,0},{12,4},{1,9},{5,13},{9,1},{13,5},{2,10},{6,14},... | collective-permute-start | bytes 1376264 | tf_op jit(solution)/shard_map/ppermute | solution.py:62
  166.3 30.8 %collective-permute-start.9 = (f32[128,896]{1,0:T(8,128)S(1)}, f32[128,896]{1,0:T(8,128)S(1)}, u32[]{:S(2)}, u32[]{:S(2)}) collective-permute-start(f32[128,896]{1,0:T(8,128)S(1)} %fusion.50), channel_id=1, source_target_pairs={{0,8},{4,12},{8,0},{12,4},{1,9},{5,13},{9,1},{13,5},{2,10},{6,14},... | collective-permute-start | bytes 1376264 | tf_op jit(solution)/shard_map/ppermute | solution.py:62
  167.6 37.7 %collective-permute-start.17 = (f32[128,896]{1,0:T(8,128)S(1)}, f32[128,896]{1,0:T(8,128)S(1)}, u32[]{:S(2)}, u32[]{:S(2)}) collective-permute-start(f32[128,896]{1,0:T(8,128)S(1)} %fusion.45), channel_id=1, source_target_pairs={{0,8},{4,12},{8,0},{12,4},{1,9},{5,13},{9,1},{13,5},{2,10},{6,14},... | collective-permute-start | bytes 1376264 | tf_op jit(solution)/shard_map/ppermute | solution.py:62
  (15 other events, 62.3 us)

commit v5 on v4

--- a/solution.py
+++ b/solution.py
@@ -74,10 +74,15 @@
         low = col < 2
         mine = col % 2 == core
         next_block = jnp.where(even, from_right[0], from_left[0])
+        first_kept = jnp.where(mine, tokens, next_block)
+        first_sent = jnp.where(mine, next_block, tokens)
+        first_kept, first_sent, tokens, near_left, near_right = lax.optimization_barrier(
+            (first_kept, first_sent, tokens, from_left[0], from_right[0])
+        )
         far_block = jnp.where(low, from_right[1], from_left[1])
         last_block = jnp.where(
             col == 0, from_right[2],
-            jnp.where(col == 1, from_right[0], jnp.where(col == 2, from_left[0], from_left[2])),
+            jnp.where(col == 1, near_right, jnp.where(col == 2, near_left, from_left[2])),
         )
 
         def stage(kept_tokens, sent_tokens):
@@ -91,7 +96,7 @@
                 pieces.append(pair + shift_hi(pair))
             return jnp.concatenate(pieces, axis=1)
 
-        first = stage(jnp.where(mine, tokens, next_block), jnp.where(mine, next_block, tokens))
+        first = stage(first_kept, first_sent)
         second = stage(jnp.where(mine, far_block, last_block), jnp.where(mine, last_block, far_block))
         shares = jnp.where(hi == col // 2, first, second)
         return shares.astype(jnp.bfloat16).reshape(block, 1, part)

time: 207 us -> 166 us (0.80)
  waiting for transfers between devices: 130 us -> 86.4 us
  starting transfers between devices: 40 us -> 45.1 us
  matrix products: 29.5 us -> 27.4 us
    ppermute x8, waiting for transfers between devices: 36.4 us -> 18.6 us  [shift_hi(): return lax.ppermute(value, 'row', pairs)]
    ppermute x8, waiting for transfers between devices: 61.3 us -> 46.6 us  [shift_depth(): return lax.ppermute(value, 'depth', pairs)]
    ppermute x3, waiting for transfers between devices: 27.4 us -> 15.7 us  [relay_tokens(): going_left = lax.ppermute(going_left, 'col', leftward)]
    ppermute x8, starting transfers between devices: 8.65 us -> 12.2 us  [shift_hi(): return lax.ppermute(value, 'row', pairs)]
    dot_general x16, matrix products: 29.5 us -> 27.4 us  [stage(): jnp.dot(both, columns(d, q), preferred_element_type=jnp.float32)]
  transfers between devices with their start and end apart: 38 -> 38, of which waited for: 22 -> 18; matrix products, arithmetic and copies ran while one was open for 4% -> 9% of each run, Pallas kernels for 0% -> 0%
where the time goes in v5:
time: 166 us; the launch traced here: 165 us
  waiting for transfers between devices  86.4 us (52%)
  starting transfers between devices  45.1 us (27%)
  matrix products  27.4 us (17%)
  other arithmetic  5.19 us (3%)
    ppermute x8, waiting for transfers between devices, shift_depth(): return lax.ppermute(value, 'depth', pairs)  46.6 us
    dot_general x16, matrix products, stage(): jnp.dot(both, columns(d, q), preferred_element_type=jnp.float32)  27.4 us
    ppermute x8, waiting for transfers between devices, shift_hi(): return lax.ppermute(value, 'row', pairs)  18.6 us
    ppermute x3, waiting for transfers between devices, relay_tokens(): going_left = lax.ppermute(going_left, 'col', leftward)  15.7 us
    ppermute x3, starting transfers between devices, relay_tokens(): going_right = lax.ppermute(going_right, 'col', rightward)  15.5 us
    ppermute x8, starting transfers between devices, shift_hi(): return lax.ppermute(value, 'row', pairs)  12.2 us
    ppermute x8, starting transfers between devices, shift_depth(): return lax.ppermute(value, 'depth', pairs)  9.81 us
    ppermute x16, waiting for transfers between devices, stage(): arrived = lax.ppermute([p[:block] for p in products], 'row', partner)  4.34 us
  transfers between devices with their start and end apart: 38, of which 18 were waited for; matrix products, arithmetic and copies ran while one was open for 9% of the time, Pallas kernels for 0%

profile of v5, /device:TPU:0, one launch (start us, length us, event | category | flops | bytes accessed | tf_op | source)
XLA Modules:
  0.0 165.4 jit_solution(16380735389639635779)
XLA Ops:
  1.3 5.6 %collective-permute-start.1 = (bf16[128,2048]{1,0:T(8,128)(2,1)}, bf16[128,2048]{1,0:T(8,128)(2,1)S(1)}, u32[]{:S(2)}, u32[]{:S(2)}) collective-permute-start(bf16[128,2048]{1,0:T(8,128)(2,1)} %param.2), channel_id=1, source_target_pairs={{0,1},{1,2},{2,3},{4,5},{5,6},{6,7},{8,9},{9,10},{10,11},{12,13},{... | collective-permute-start | bytes 1572872 | tf_op jit(solution)/shard_map/ppermute | solution.py:24
  7.0 10.1 %collective-permute-done = bf16[128,2048]{1,0:T(8,128)(2,1)S(1)} collective-permute-done((bf16[128,2048]{1,0:T(8,128)(2,1)}, bf16[128,2048]{1,0:T(8,128)(2,1)S(1)}, u32[]{:S(2)}, u32[]{:S(2)}) %collective-permute-start) | collective-permute-done | bytes 524320 | tf_op jit(solution)/shard_map/ppermute | solution.py:25
  19.6 3.5 %fusion.6 = f32[256,896]{1,0:T(8,128)S(1)} fusion(bf16[256,2048]{1,0:T(8,128)(2,1)S(1)} %constant_dynamic-update-slice_fusion, bf16[2048,6656]{1,0:T(8,128)(2,1)} %param.3), kind=kOutput, calls=%fused_computation.6 | convolution fusion | flops 939524096 | bytes 5636096 | tf_op jit(solution)/shard_map/dot_general | solution.py:92
  23.1 4.1 %fusion.2 = f32[256,896]{1,0:T(8,128)S(1)} fusion(bf16[256,2048]{1,0:T(8,128)(2,1)S(1)} %constant_dynamic-update-slice_fusion, bf16[2048,6656]{1,0:T(8,128)(2,1)} %param.3), kind=kOutput, calls=%fused_computation.2 | convolution fusion | flops 939524096 | bytes 5636096 | tf_op jit(solution)/shard_map/dot_general | solution.py:92
  27.1 3.6 %fusion.22 = f32[256,768]{1,0:T(8,128)S(1)} fusion(bf16[256,2048]{1,0:T(8,128)(2,1)S(1)} %constant_dynamic-update-slice_fusion, bf16[2048,6656]{1,0:T(8,128)(2,1)} %param.3), kind=kOutput, calls=%fused_computation.22 | convolution fusion | flops 805306368 | bytes 4980736 | tf_op jit(solution)/shard_map/dot_general | solution.py:92
  30.8 2.9 %fusion.18 = f32[256,768]{1,0:T(8,128)S(1)} fusion(bf16[256,2048]{1,0:T(8,128)(2,1)S(1)} %constant_dynamic-update-slice_fusion, bf16[2048,6656]{1,0:T(8,128)(2,1)} %param.3), kind=kOutput, calls=%fused_computation.18 | convolution fusion | flops 805306368 | bytes 4980736 | tf_op jit(solution)/shard_map/dot_general | solution.py:92
  40.6 2.1 %collective-permute-done.2 = f32[128,768]{1,0:T(8,128)S(1)} collective-permute-done((f32[128,768]{1,0:T(8,128)S(1)}, f32[128,768]{1,0:T(8,128)S(1)}, u32[]{:S(2)}, u32[]{:S(2)}) %collective-permute-start.2) | collective-permute-done | bytes 393248 | tf_op jit(solution)/shard_map/ppermute | solution.py:93
  44.8 4.9 %collective-permute-start.20 = (bf16[128,2048]{1,0:T(8,128)(2,1)S(1)}, bf16[128,2048]{1,0:T(8,128)(2,1)S(1)}, u32[]{:S(2)}, u32[]{:S(2)}) collective-permute-start(bf16[128,2048]{1,0:T(8,128)(2,1)S(1)} %collective-permute-done.1), channel_id=1, source_target_pairs={{0,1},{1,2},{2,3},{4,5},{5,6},{6,7},{8,9},{9,10},{10,11},{12,13},{... | collective-permute-start | bytes 1572872 | tf_op jit(solution)/shard_map/ppermute | solution.py:24
  49.8 1.7 %collective-permute-start.12 = (f32[128,768]{1,0:T(8,128)S(1)}, f32[128,768]{1,0:T(8,128)S(1)}, u32[]{:S(2)}, u32[]{:S(2)}) collective-permute-start(f32[128,768]{1,0:T(8,128)S(1)} %fusion.75), channel_id=1, source_target_pairs={{0,16},{16,0},{1,17},{17,1},{2,18},{18,2},{3,19},{19,3},{4,20},{20... | collective-permute-start | bytes 1179656 | tf_op jit(solution)/shard_map/ppermute | solution.py:66
  52.2 1.7 %collective-permute-start.16 = (f32[128,896]{1,0:T(8,128)S(1)}, f32[128,896]{1,0:T(8,128)S(1)}, u32[]{:S(2)}, u32[]{:S(2)}) collective-permute-start(f32[128,896]{1,0:T(8,128)S(1)} %fusion.47), channel_id=1, source_target_pairs={{0,16},{16,0},{1,17},{17,1},{2,18},{18,2},{3,19},{19,3},{4,20},{20... | collective-permute-start | bytes 1376264 | tf_op jit(solution)/shard_map/ppermute | solution.py:66
  54.1 5.6 %collective-permute-done.18 = bf16[128,2048]{1,0:T(8,128)(2,1)S(1)} collective-permute-done((bf16[128,2048]{1,0:T(8,128)(2,1)S(1)}, bf16[128,2048]{1,0:T(8,128)(2,1)S(1)}, u32[]{:S(2)}, u32[]{:S(2)}) %collective-permute-start.18) | collective-permute-done | bytes 524320 | tf_op jit(solution)/shard_map/ppermute | solution.py:25
  62.7 5.0 %collective-permute-start.21 = (bf16[128,2048]{1,0:T(8,128)(2,1)S(1)}, bf16[128,2048]{1,0:T(8,128)(2,1)S(1)}, u32[]{:S(2)}, u32[]{:S(2)}) collective-permute-start(bf16[128,2048]{1,0:T(8,128)(2,1)S(1)} %collective-permute-done.20), channel_id=1, source_target_pairs={{0,1},{1,2},{2,3},{4,5},{5,6},{6,7},{8,9},{9,10},{10,11},{12,13},{... | collective-permute-start | bytes 1572872 | tf_op jit(solution)/shard_map/ppermute | solution.py:24
  67.8 2.5 %collective-permute-done.4 = f32[128,768]{1,0:T(8,128)S(1)} collective-permute-done((f32[128,768]{1,0:T(8,128)S(1)}, f32[128,768]{1,0:T(8,128)S(1)}, u32[]{:S(2)}, u32[]{:S(2)}) %collective-permute-start.4) | collective-permute-done | bytes 393248 | tf_op jit(solution)/shard_map/ppermute | solution.py:66
  72.0 8.1 %collective-permute-done.16 = f32[128,896]{1,0:T(8,128)S(1)} collective-permute-done((f32[128,896]{1,0:T(8,128)S(1)}, f32[128,896]{1,0:T(8,128)S(1)}, u32[]{:S(2)}, u32[]{:S(2)}) %collective-permute-start.16) | collective-permute-done | bytes 458784 | tf_op jit(solution)/shard_map/ppermute | solution.py:66
  81.9 7.0 %collective-permute-done.8 = f32[128,896]{1,0:T(8,128)S(1)} collective-permute-done((f32[128,896]{1,0:T(8,128)S(1)}, f32[128,896]{1,0:T(8,128)S(1)}, u32[]{:S(2)}, u32[]{:S(2)}) %collective-permute-start.8) | collective-permute-done | bytes 458784 | tf_op jit(solution)/shard_map/ppermute | solution.py:66
  102.3 7.8 %collective-permute-done.9 = f32[128,896]{1,0:T(8,128)S(1)} collective-permute-done((f32[128,896]{1,0:T(8,128)S(1)}, f32[128,896]{1,0:T(8,128)S(1)}, u32[]{:S(2)}, u32[]{:S(2)}) %collective-permute-start.9) | collective-permute-done | bytes 458784 | tf_op jit(solution)/shard_map/ppermute | solution.py:62
  115.5 1.7 %collective-permute-start.36 = (f32[128,896]{1,0:T(8,128)S(1)}, f32[128,896]{1,0:T(8,128)S(1)}, u32[]{:S(2)}, u32[]{:S(2)}) collective-permute-start(f32[128,896]{1,0:T(8,128)S(1)} %fusion.37), channel_id=1, source_target_pairs={{0,16},{16,0},{1,17},{17,1},{2,18},{18,2},{3,19},{19,3},{4,20},{20... | collective-permute-start | bytes 1376264 | tf_op jit(solution)/shard_map/ppermute | solution.py:66
  117.9 7.1 %collective-permute-done.32 = f32[128,768]{1,0:T(8,128)S(1)} collective-permute-done((f32[128,768]{1,0:T(8,128)S(1)}, f32[128,768]{1,0:T(8,128)S(1)}, u32[]{:S(2)}, u32[]{:S(2)}) %collective-permute-start.32) | collective-permute-done | bytes 393248 | tf_op jit(solution)/shard_map/ppermute | solution.py:66
  125.1 1.7 %collective-permute-start.33 = (f32[128,768]{1,0:T(8,128)S(1)}, f32[128,768]{1,0:T(8,128)S(1)}, u32[]{:S(2)}, u32[]{:S(2)}) collective-permute-start(f32[128,768]{1,0:T(8,128)S(1)} %fusion.63), channel_id=1, source_target_pairs={{0,8},{4,12},{8,0},{12,4},{1,9},{5,13},{9,1},{13,5},{2,10},{6,14},... | collective-permute-start | bytes 1179656 | tf_op jit(solution)/shard_map/ppermute | solution.py:62
  126.8 6.6 %collective-permute-done.24 = f32[128,768]{1,0:T(8,128)S(1)} collective-permute-done((f32[128,768]{1,0:T(8,128)S(1)}, f32[128,768]{1,0:T(8,128)S(1)}, u32[]{:S(2)}, u32[]{:S(2)}) %collective-permute-start.24) | collective-permute-done | bytes 393248 | tf_op jit(solution)/shard_map/ppermute | solution.py:66
  135.2 8.0 %collective-permute-done.36 = f32[128,896]{1,0:T(8,128)S(1)} collective-permute-done((f32[128,896]{1,0:T(8,128)S(1)}, f32[128,896]{1,0:T(8,128)S(1)}, u32[]{:S(2)}, u32[]{:S(2)}) %collective-permute-start.36) | collective-permute-done | bytes 458784 | tf_op jit(solution)/shard_map/ppermute | solution.py:66
  143.4 1.7 %collective-permute-start.37 = (f32[128,896]{1,0:T(8,128)S(1)}, f32[128,896]{1,0:T(8,128)S(1)}, u32[]{:S(2)}, u32[]{:S(2)}) collective-permute-start(f32[128,896]{1,0:T(8,128)S(1)} %fusion.35), channel_id=1, source_target_pairs={{0,8},{4,12},{8,0},{12,4},{1,9},{5,13},{9,1},{13,5},{2,10},{6,14},... | collective-permute-start | bytes 1376264 | tf_op jit(solution)/shard_map/ppermute | solution.py:62
  145.1 7.2 %collective-permute-done.28 = f32[128,896]{1,0:T(8,128)S(1)} collective-permute-done((f32[128,896]{1,0:T(8,128)S(1)}, f32[128,896]{1,0:T(8,128)S(1)}, u32[]{:S(2)}, u32[]{:S(2)}) %collective-permute-start.28) | collective-permute-done | bytes 458784 | tf_op jit(solution)/shard_map/ppermute | solution.py:66
  154.4 9.8 %collective-permute-done.29 = f32[128,896]{1,0:T(8,128)S(1)} collective-permute-done((f32[128,896]{1,0:T(8,128)S(1)}, f32[128,896]{1,0:T(8,128)S(1)}, u32[]{:S(2)}, u32[]{:S(2)}) %collective-permute-start.29) | collective-permute-done | bytes 458784 | tf_op jit(solution)/shard_map/ppermute | solution.py:62
  (132 shorter events, 44.5 us)
Async XLA Ops:
  0.0 17.1 %collective-permute-start = (bf16[128,2048]{1,0:T(8,128)(2,1)}, bf16[128,2048]{1,0:T(8,128)(2,1)S(1)}, u32[]{:S(2)}, u32[]{:S(2)}) collective-permute-start(bf16[128,2048]{1,0:T(8,128)(2,1)} %param.2), channel_id=1, source_target_pairs={{1,0},{2,1},{3,2},{5,4},{6,5},{7,6},{9,8},{10,9},{11,10},{13,12},{... | collective-permute-start | bytes 1572872 | tf_op jit(solution)/shard_map/ppermute | solution.py:25
  1.3 17.1 %collective-permute-start.1 = (bf16[128,2048]{1,0:T(8,128)(2,1)}, bf16[128,2048]{1,0:T(8,128)(2,1)S(1)}, u32[]{:S(2)}, u32[]{:S(2)}) collective-permute-start(bf16[128,2048]{1,0:T(8,128)(2,1)} %param.2), channel_id=1, source_target_pairs={{0,1},{1,2},{2,3},{4,5},{5,6},{6,7},{8,9},{9,10},{10,11},{12,13},{... | collective-permute-start | bytes 1572872 | tf_op jit(solution)/shard_map/ppermute | solution.py:24
  39.6 12.0 %collective-permute-start.6 = (f32[128,896]{1,0:T(8,128)S(1)}, f32[128,896]{1,0:T(8,128)S(1)}, u32[]{:S(2)}, u32[]{:S(2)}) collective-permute-start(f32[128,896]{1,0:T(8,128)S(1)} %slice.173), channel_id=1, source_target_pairs={{0,4},{4,0},{8,12},{12,8},{1,5},{5,1},{9,13},{13,9},{2,6},{6,2},{1... | collective-permute-start | bytes 1376264 | tf_op jit(solution)/shard_map/ppermute | solution.py:93
  43.2 16.5 %collective-permute-start.18 = (bf16[128,2048]{1,0:T(8,128)(2,1)S(1)}, bf16[128,2048]{1,0:T(8,128)(2,1)S(1)}, u32[]{:S(2)}, u32[]{:S(2)}) collective-permute-start(bf16[128,2048]{1,0:T(8,128)(2,1)S(1)} %collective-permute-done), channel_id=1, source_target_pairs={{1,0},{2,1},{3,2},{5,4},{6,5},{7,6},{9,8},{10,9},{11,10},{13,12},{... | collective-permute-start | bytes 1572872 | tf_op jit(solution)/shard_map/ppermute | solution.py:25
  44.8 16.6 %collective-permute-start.20 = (bf16[128,2048]{1,0:T(8,128)(2,1)S(1)}, bf16[128,2048]{1,0:T(8,128)(2,1)S(1)}, u32[]{:S(2)}, u32[]{:S(2)}) collective-permute-start(bf16[128,2048]{1,0:T(8,128)(2,1)S(1)} %collective-permute-done.1), channel_id=1, source_target_pairs={{0,1},{1,2},{2,3},{4,5},{5,6},{6,7},{8,9},{9,10},{10,11},{12,13},{... | collective-permute-start | bytes 1572872 | tf_op jit(solution)/shard_map/ppermute | solution.py:24
  49.8 12.9 %collective-permute-start.12 = (f32[128,768]{1,0:T(8,128)S(1)}, f32[128,768]{1,0:T(8,128)S(1)}, u32[]{:S(2)}, u32[]{:S(2)}) collective-permute-start(f32[128,768]{1,0:T(8,128)S(1)} %fusion.75), channel_id=1, source_target_pairs={{0,16},{16,0},{1,17},{17,1},{2,18},{18,2},{3,19},{19,3},{4,20},{20... | collective-permute-start | bytes 1179656 | tf_op jit(solution)/shard_map/ppermute | solution.py:66
  51.6 18.7 %collective-permute-start.4 = (f32[128,768]{1,0:T(8,128)S(1)}, f32[128,768]{1,0:T(8,128)S(1)}, u32[]{:S(2)}, u32[]{:S(2)}) collective-permute-start(f32[128,768]{1,0:T(8,128)S(1)} %fusion.80), channel_id=1, source_target_pairs={{0,16},{16,0},{1,17},{17,1},{2,18},{18,2},{3,19},{19,3},{4,20},{20... | collective-permute-start | bytes 1179656 | tf_op jit(solution)/shard_map/ppermute | solution.py:66
  52.2 27.9 %collective-permute-start.16 = (f32[128,896]{1,0:T(8,128)S(1)}, f32[128,896]{1,0:T(8,128)S(1)}, u32[]{:S(2)}, u32[]{:S(2)}) collective-permute-start(f32[128,896]{1,0:T(8,128)S(1)} %fusion.47), channel_id=1, source_target_pairs={{0,16},{16,0},{1,17},{17,1},{2,18},{18,2},{3,19},{19,3},{4,20},{20... | collective-permute-start | bytes 1376264 | tf_op jit(solution)/shard_map/ppermute | solution.py:66
  59.7 29.1 %collective-permute-start.8 = (f32[128,896]{1,0:T(8,128)S(1)}, f32[128,896]{1,0:T(8,128)S(1)}, u32[]{:S(2)}, u32[]{:S(2)}) collective-permute-start(f32[128,896]{1,0:T(8,128)S(1)} %fusion.52), channel_id=1, source_target_pairs={{0,16},{16,0},{1,17},{17,1},{2,18},{18,2},{3,19},{19,3},{4,20},{20... | collective-permute-start | bytes 1376264 | tf_op jit(solution)/shard_map/ppermute | solution.py:66
  61.4 29.2 %collective-permute-start.19 = (bf16[128,2048]{1,0:T(8,128)(2,1)S(1)}, bf16[128,2048]{1,0:T(8,128)(2,1)S(1)}, u32[]{:S(2)}, u32[]{:S(2)}) collective-permute-start(bf16[128,2048]{1,0:T(8,128)(2,1)S(1)} %collective-permute-done.18), channel_id=1, source_target_pairs={{1,0},{2,1},{3,2},{5,4},{6,5},{7,6},{9,8},{10,9},{11,10},{13,12},{... | collective-permute-start | bytes 1572872 | tf_op jit(solution)/shard_map/ppermute | solution.py:25
  62.7 28.3 %collective-permute-start.21 = (bf16[128,2048]{1,0:T(8,128)(2,1)S(1)}, bf16[128,2048]{1,0:T(8,128)(2,1)S(1)}, u32[]{:S(2)}, u32[]{:S(2)}) collective-permute-start(bf16[128,2048]{1,0:T(8,128)(2,1)S(1)} %collective-permute-done.20), channel_id=1, source_target_pairs={{0,1},{1,2},{2,3},{4,5},{5,6},{6,7},{8,9},{9,10},{10,11},{12,13},{... | collective-permute-start | bytes 1572872 | tf_op jit(solution)/shard_map/ppermute | solution.py:24
  70.3 30.4 %collective-permute-start.13 = (f32[128,768]{1,0:T(8,128)S(1)}, f32[128,768]{1,0:T(8,128)S(1)}, u32[]{:S(2)}, u32[]{:S(2)}) collective-permute-start(f32[128,768]{1,0:T(8,128)S(1)} %fusion.73), channel_id=1, source_target_pairs={{0,8},{4,12},{8,0},{12,4},{1,9},{5,13},{9,1},{13,5},{2,10},{6,14},... | collective-permute-start | bytes 1179656 | tf_op jit(solution)/shard_map/ppermute | solution.py:62
  80.1 21.2 %collective-permute-start.5 = (f32[128,768]{1,0:T(8,128)S(1)}, f32[128,768]{1,0:T(8,128)S(1)}, u32[]{:S(2)}, u32[]{:S(2)}) collective-permute-start(f32[128,768]{1,0:T(8,128)S(1)} %fusion.78), channel_id=1, source_target_pairs={{0,8},{4,12},{8,0},{12,4},{1,9},{5,13},{9,1},{13,5},{2,10},{6,14},... | collective-permute-start | bytes 1179656 | tf_op jit(solution)/shard_map/ppermute | solution.py:62
  88.8 13.4 %collective-permute-start.17 = (f32[128,896]{1,0:T(8,128)S(1)}, f32[128,896]{1,0:T(8,128)S(1)}, u32[]{:S(2)}, u32[]{:S(2)}) collective-permute-start(f32[128,896]{1,0:T(8,128)S(1)} %fusion.45), channel_id=1, source_target_pairs={{0,8},{4,12},{8,0},{12,4},{1,9},{5,13},{9,1},{13,5},{2,10},{6,14},... | collective-permute-start | bytes 1376264 | tf_op jit(solution)/shard_map/ppermute | solution.py:62
  90.6 19.5 %collective-permute-start.9 = (f32[128,896]{1,0:T(8,128)S(1)}, f32[128,896]{1,0:T(8,128)S(1)}, u32[]{:S(2)}, u32[]{:S(2)}) collective-permute-start(f32[128,896]{1,0:T(8,128)S(1)} %fusion.50), channel_id=1, source_target_pairs={{0,8},{4,12},{8,0},{12,4},{1,9},{5,13},{9,1},{13,5},{2,10},{6,14},... | collective-permute-start | bytes 1376264 | tf_op jit(solution)/shard_map/ppermute | solution.py:62
  100.3 14.5 %collective-permute-start.34 = (f32[128,896]{1,0:T(8,128)S(1)}, f32[128,896]{1,0:T(8,128)S(1)}, u32[]{:S(2)}, u32[]{:S(2)}) collective-permute-start(f32[128,896]{1,0:T(8,128)S(1)} %slice.197), channel_id=1, source_target_pairs={{0,4},{4,0},{8,12},{12,8},{1,5},{5,1},{9,13},{13,9},{2,6},{6,2},{1... | collective-permute-start | bytes 1376264 | tf_op jit(solution)/shard_map/ppermute | solution.py:93
  100.7 14.7 %collective-permute-start.35 = (f32[128,896]{1,0:T(8,128)S(1)}, f32[128,896]{1,0:T(8,128)S(1)}, u32[]{:S(2)}, u32[]{:S(2)}) collective-permute-start(f32[128,896]{1,0:T(8,128)S(1)} %slice.199), channel_id=1, source_target_pairs={{0,4},{4,0},{8,12},{12,8},{1,5},{5,1},{9,13},{13,9},{2,6},{6,2},{1... | collective-permute-start | bytes 1376264 | tf_op jit(solution)/shard_map/ppermute | solution.py:93
  113.0 12.0 %collective-permute-start.32 = (f32[128,768]{1,0:T(8,128)S(1)}, f32[128,768]{1,0:T(8,128)S(1)}, u32[]{:S(2)}, u32[]{:S(2)}) collective-permute-start(f32[128,768]{1,0:T(8,128)S(1)} %fusion.65), channel_id=1, source_target_pairs={{0,16},{16,0},{1,17},{17,1},{2,18},{18,2},{3,19},{19,3},{4,20},{20... | collective-permute-start | bytes 1179656 | tf_op jit(solution)/shard_map/ppermute | solution.py:66
  114.9 18.6 %collective-permute-start.24 = (f32[128,768]{1,0:T(8,128)S(1)}, f32[128,768]{1,0:T(8,128)S(1)}, u32[]{:S(2)}, u32[]{:S(2)}) collective-permute-start(f32[128,768]{1,0:T(8,128)S(1)} %fusion.70), channel_id=1, source_target_pairs={{0,16},{16,0},{1,17},{17,1},{2,18},{18,2},{3,19},{19,3},{4,20},{20... | collective-permute-start | bytes 1179656 | tf_op jit(solution)/shard_map/ppermute | solution.py:66
  115.5 27.8 %collective-permute-start.36 = (f32[128,896]{1,0:T(8,128)S(1)}, f32[128,896]{1,0:T(8,128)S(1)}, u32[]{:S(2)}, u32[]{:S(2)}) collective-permute-start(f32[128,896]{1,0:T(8,128)S(1)} %fusion.37), channel_id=1, source_target_pairs={{0,16},{16,0},{1,17},{17,1},{2,18},{18,2},{3,19},{19,3},{4,20},{20... | collective-permute-start | bytes 1376264 | tf_op jit(solution)/shard_map/ppermute | solution.py:66
  117.5 34.8 %collective-permute-start.28 = (f32[128,896]{1,0:T(8,128)S(1)}, f32[128,896]{1,0:T(8,128)S(1)}, u32[]{:S(2)}, u32[]{:S(2)}) collective-permute-start(f32[128,896]{1,0:T(8,128)S(1)} %fusion.42), channel_id=1, source_target_pairs={{0,16},{16,0},{1,17},{17,1},{2,18},{18,2},{3,19},{19,3},{4,20},{20... | collective-permute-start | bytes 1376264 | tf_op jit(solution)/shard_map/ppermute | solution.py:66
  125.1 29.0 %collective-permute-start.33 = (f32[128,768]{1,0:T(8,128)S(1)}, f32[128,768]{1,0:T(8,128)S(1)}, u32[]{:S(2)}, u32[]{:S(2)}) collective-permute-start(f32[128,768]{1,0:T(8,128)S(1)} %fusion.63), channel_id=1, source_target_pairs={{0,8},{4,12},{8,0},{12,4},{1,9},{5,13},{9,1},{13,5},{2,10},{6,14},... | collective-permute-start | bytes 1179656 | tf_op jit(solution)/shard_map/ppermute | solution.py:62
  133.5 20.7 %collective-permute-start.25 = (f32[128,768]{1,0:T(8,128)S(1)}, f32[128,768]{1,0:T(8,128)S(1)}, u32[]{:S(2)}, u32[]{:S(2)}) collective-permute-start(f32[128,768]{1,0:T(8,128)S(1)} %fusion.68), channel_id=1, source_target_pairs={{0,8},{4,12},{8,0},{12,4},{1,9},{5,13},{9,1},{13,5},{2,10},{6,14},... | collective-permute-start | bytes 1179656 | tf_op jit(solution)/shard_map/ppermute | solution.py:62
  152.4 11.8 %collective-permute-start.29 = (f32[128,896]{1,0:T(8,128)S(1)}, f32[128,896]{1,0:T(8,128)S(1)}, u32[]{:S(2)}, u32[]{:S(2)}) collective-permute-start(f32[128,896]{1,0:T(8,128)S(1)} %fusion.40), channel_id=1, source_target_pairs={{0,8},{4,12},{8,0},{12,4},{1,9},{5,13},{9,1},{13,5},{2,10},{6,14},... | collective-permute-start | bytes 1376264 | tf_op jit(solution)/shard_map/ppermute | solution.py:62
  (15 other events, 97.6 us)
